TPU v7x, 32 devices: a whole 2x2x4 slice. The times are simulated.
32 devices in a mesh: grp: 2 (over x), section: 16 (over z, y, core).
Axes of the slice: x: 2, y: 2, z: 4, core: 2. Of those that a mesh axis runs over, the one named last changes fastest.
Arguments:
- latent: bfloat16 [1536, 64], P(('grp', 'section')), parts along dimension 0, may hold values from -6 to 6
- control_latent: bfloat16 [1536, 64], P(('grp', 'section')), parts along dimension 0, may hold values from -6 to 6
- patch_tiles: int32 [4], replicated, may hold values from 1 to 2, 6 in all
- tile_lists: int32 [2, 6, 3], replicated, may hold values from 0 to 5, as said below
- tile_counts: int32 [2, 6], replicated, may hold values from 1 to 3, as said below
- embed_weight: bfloat16 [64, 3072], replicated, may hold values from -0.75 to 0.75
- control_embed: bfloat16 [64, 3072], replicated, may hold values from -0.75 to 0.75
- modulation: float32 [2, 3, 3072], replicated, may hold values from -4 to 4
- qk_gain: float32 [2, 2, 128], replicated, may hold values from 0.1 to 1.9
- qkv_weight: bfloat16 [16, 3072, 1152], P('section'), may hold values from -0.109375 to 0.109375
- out_weight: bfloat16 [16, 384, 3072], P('section'), may hold values from -0.109375 to 0.109375
- stale_cache: bfloat16 [16, 1536, 768], P('section', 'grp'), parts along dimension 1, may hold values from -6 to 6
- control_gain: float32 [1, 3072], replicated, may hold values from -3 to 3
- final_mod: float32 [2, 3072], replicated, may hold values from -3 to 3
- final_weight: bfloat16 [3072, 64], replicated, may hold values from -0.109375 to 0.109375
Outputs:
- denoised: float32 [1536, 64], P(('grp', 'section')), parts along dimension 0
There are 2 independent parts, one for each index of `grp`. A program takes and returns all parts, laid end to end along the dimension named above; an argument that names none is the same for every part. Nothing has to cross between parts.
Inputs may be any that keep to these rules, and one draw needn't show every extreme that they name: `patch_tiles`: the patches are contiguous and in order and together cover all 6 tiles; the largest has exactly 2 tiles. Entry 0 of tile_lists[b, t] is t itself; the 3 entries of one row are distinct. `tile_counts`: in every block slot some query tile uses all 3 listed tiles.
All inputs are finite; a program needn't handle non-finite values.
Results may differ from a plain program's by a relative error of at most 0.014.
Values may be sent and summed in bfloat16 or wider, within the bound.
No kernel may reach another device: no remote copies, remote signals or barrier semaphores. Data moves between devices by JAX's collectives and lax.ppermute only.
A program may use at most 64 MiB of HBM per device.

v0:
```python
import math

import jax
import jax.numpy as jnp
from jax import lax
from jax.sharding import PartitionSpec as P

D = 3072
HD = 128
HG = 8
C_OUT = 64
TILE = 128
KSEL = 3
PATCHES = 4
TILES = 6
PMAX = 2


EPSILON = 1e-06


def from_partner(value, axis, distance):
    return lax.ppermute(value, axis, [(i, i ^ 1 << distance) for i in range(lax.axis_size(axis))])


def from_behind(value, axis, steps):
    count = lax.axis_size(axis)
    leading, last = (max(0, -steps), min(count, count - steps))
    return lax.ppermute(value, axis, [(source, source + steps) for source in range(leading, last)])


def modulated(hidden, shift_row, scale_row):
    values = hidden.astype(jnp.float32)
    centered = values - jnp.mean(values, axis=-1, keepdims=True)
    variance = jnp.mean(centered * centered, axis=-1, keepdims=True)
    normed = centered * lax.rsqrt(variance + EPSILON)
    return (normed * (1.0 + scale_row) + shift_row).astype(jnp.bfloat16)


def rms_scaled(values, gain_row):
    return (
        values * lax.rsqrt(jnp.mean(values * values, axis=-1, keepdims=True) + EPSILON) * gain_row
    )


def attend_group(
    modded, w_qkv, w_out, memory, gain_pair, start_tile, patch_length, tile_list, tile_limit
):
    row_count = modded.shape[0]
    query_tiles_count = row_count // TILE
    head_count = w_out.shape[0] // HD
    projected = jnp.dot(modded, w_qkv, preferred_element_type=jnp.float32).reshape(
        row_count, 3, head_count, HD
    )
    queries = rms_scaled(projected[:, 0], gain_pair[0]).astype(jnp.bfloat16)
    keys_new = rms_scaled(projected[:, 1], gain_pair[1]).astype(jnp.bfloat16)
    values_new = projected[:, 2].astype(jnp.bfloat16)
    fresh_rows = jnp.concatenate(
        [
            keys_new.reshape(row_count, head_count * HD),
            values_new.reshape(row_count, head_count * HD),
        ],
        axis=1,
    )
    row_start = start_tile * TILE
    previous = lax.dynamic_slice_in_dim(memory, row_start, row_count, 0)
    live_rows = jnp.arange(row_count) < patch_length * TILE
    memory = lax.dynamic_update_slice_in_dim(
        memory, jnp.where(live_rows[:, None], fresh_rows, previous), row_start, 0
    )
    tiled_memory = memory.reshape(-1, TILE, 2, head_count, HD)
    query_tiles = jnp.minimum(start_tile + jnp.arange(query_tiles_count), TILES - 1)
    picked = tile_list[query_tiles]
    used_counts = tile_limit[query_tiles]
    chosen = tiled_memory[picked]
    key_rows = chosen[:, :, :, 0].reshape(query_tiles_count, KSEL * TILE, head_count, HD)
    value_rows = chosen[:, :, :, 1].reshape(query_tiles_count, KSEL * TILE, head_count, HD)
    query_rows = queries.reshape(query_tiles_count, TILE, head_count, HD)
    scores = jnp.einsum(
        "tqhd,tkhd->thqk", query_rows, key_rows, preferred_element_type=jnp.float32
    ) / math.sqrt(HD)
    allowed = (jnp.arange(KSEL * TILE) // TILE)[None, :] < used_counts[:, None]
    scores = jnp.where(allowed[:, None, None, :], scores, -1e30)
    highest = jnp.max(scores, axis=-1, keepdims=True)
    weights = jnp.exp(scores - highest)
    probabilities = (weights / jnp.sum(weights, axis=-1, keepdims=True)).astype(jnp.bfloat16)
    attended = jnp.einsum(
        "thqk,tkhd->tqhd", probabilities, value_rows, preferred_element_type=jnp.float32
    ).astype(jnp.bfloat16)
    attended = attended.reshape(row_count, head_count * HD)
    partial_value = jnp.dot(attended, w_out, preferred_element_type=jnp.float32)
    return (partial_value, memory)


def split_rows(current, upper_half):
    middle = current.shape[0] // 2
    kept = jnp.where(upper_half, current[middle:], current[:middle])
    given = jnp.where(upper_half, current[:middle], current[middle:])
    return (kept, given)


def on_device(
    latent,
    control_latent,
    patch_tiles,
    tile_lists,
    tile_counts,
    embed_weight,
    control_embed,
    modulation,
    qk_gain,
    qkv_weight,
    out_weight,
    stale_cache,
    control_gain,
    final_mod,
    final_weight,
):
    slot_count = lax.axis_size("section") // HG
    control_count = slot_count // 2
    device_index = lax.axis_index("section")
    slot_index = device_index // HG
    group_index = device_index % HG
    is_control = slot_index % 2 == 0
    chain_index = slot_index // 2
    row_count = PMAX * TILE
    share_rows = row_count // HG
    bit_count = HG.bit_length() - 1
    bit_order = list(range(bit_count - 1, -1, -1))
    share_start = jnp.zeros((), jnp.int32)
    for position, bit_index in enumerate(bit_order):
        share_start = share_start + (group_index >> bit_index & 1) * (row_count >> position + 1)
    whole_latent, whole_control = (
        lax.all_gather(latent, "section", axis=0, tiled=True),
        lax.all_gather(control_latent, "section", axis=0, tiled=True),
    )
    padding = ((0, row_count), (0, 0))
    latent_pad = jnp.pad(whole_latent, padding)
    control_pad = jnp.pad(whole_control, padding)
    seq_rows = whole_latent.shape[0]
    memory_start = jnp.pad(stale_cache[0], padding)
    w_qkv = qkv_weight[0]
    w_out = out_weight[0]
    shifts = modulation[slot_index]
    gain_pair = qk_gain[slot_index]
    tile_list = tile_lists[slot_index]
    tile_limit = tile_counts[slot_index]
    control_row = control_gain[jnp.minimum(chain_index, control_count - 1)]
    is_last_main = slot_index == slot_count - 1
    starts = jnp.cumsum(patch_tiles) - patch_tiles

    def reduce_share(partial_value):
        upper_half = group_index >> bit_order[0] & 1 == 1
        kept, given = split_rows(partial_value.astype(jnp.bfloat16), upper_half)
        summed = kept.astype(jnp.float32) + from_partner(given, "section", bit_order[0]).astype(
            jnp.float32
        )
        for bit_index in bit_order[1:]:
            upper_half = group_index >> bit_index & 1 == 1
            kept, given = split_rows(summed, upper_half)
            summed = kept + from_partner(given.astype(jnp.bfloat16), "section", bit_index).astype(
                given.dtype
            )
        return summed

    def gather_rows(gathered):
        for bit_index in reversed(bit_order):
            partner = from_partner(gathered, "section", bit_index)
            upper_half = group_index >> bit_index & 1 == 1
            gathered = jnp.where(
                upper_half,
                jnp.concatenate([partner, gathered]),
                jnp.concatenate([gathered, partner]),
            )
        return gathered

    def run_tick(tick_index, carry):
        inflow_hidden, inflow_control, memory, denoised = carry
        patch_index = tick_index - slot_index
        active = (patch_index >= 0) & (patch_index < PATCHES)
        patch_index = jnp.clip(patch_index, 0, PATCHES - 1)
        start_tile = starts[patch_index]
        patch_length = patch_tiles[patch_index]
        row_start = start_tile * TILE + share_start
        own_latent = lax.dynamic_slice_in_dim(latent_pad, row_start, share_rows, 0)
        own_control = lax.dynamic_slice_in_dim(control_pad, row_start, share_rows, 0)
        embedded = jnp.dot(own_latent, embed_weight, preferred_element_type=jnp.float32)
        conditioned = embedded + jnp.dot(
            own_control, control_embed, preferred_element_type=jnp.float32
        )
        first_slot = slot_index == 0
        current_hidden = jnp.where(first_slot, embedded.astype(jnp.bfloat16), inflow_hidden)
        current_control = jnp.where(first_slot, conditioned.astype(jnp.bfloat16), inflow_control)
        stream = jnp.where(is_control, current_control, current_hidden)
        gathered = gather_rows(stream)

        def compute(memory_in):
            modded = modulated(gathered, shifts[0], shifts[1])
            return attend_group(
                modded,
                w_qkv,
                w_out,
                memory_in,
                gain_pair,
                start_tile,
                patch_length,
                tile_list,
                tile_limit,
            )

        def skipped(memory_in):
            return (jnp.zeros((row_count, w_out.shape[1]), jnp.float32), memory_in)

        partial_value, memory = lax.cond(active, compute, skipped, memory)
        summed = reduce_share(partial_value)
        updated = stream.astype(jnp.float32) + shifts[2] * summed
        new_control = updated.astype(jnp.bfloat16)
        new_hidden = (updated + control_row * current_control.astype(jnp.float32)).astype(
            jnp.bfloat16
        )
        out_hidden = jnp.where(is_control, current_hidden, new_hidden)
        out_control = jnp.where(is_control, new_control, current_control)
        final_rows = jnp.dot(
            modulated(out_hidden, final_mod[0], final_mod[1]),
            final_weight,
            preferred_element_type=jnp.float32,
        )
        live_rows = (
            active & is_last_main & (share_start + jnp.arange(share_rows) < patch_length * TILE)
        )
        previous = lax.dynamic_slice_in_dim(denoised, row_start, share_rows, 0)
        denoised = lax.dynamic_update_slice_in_dim(
            denoised, jnp.where(live_rows[:, None], final_rows, previous), row_start, 0
        )
        inflow_hidden, inflow_control = from_behind((out_hidden, out_control), "section", HG)
        return (inflow_hidden, inflow_control, memory, denoised)

    empty_share = jnp.zeros((share_rows, D), jnp.bfloat16)
    initial = (
        empty_share,
        empty_share,
        memory_start,
        jnp.zeros((seq_rows + row_count, C_OUT), jnp.float32),
    )
    finished = lax.fori_loop(0, slot_count + PATCHES - 1, run_tick, initial)
    return lax.psum_scatter(finished[3][:seq_rows], "section", scatter_dimension=0, tiled=True)


def solution(mesh):
    return jax.shard_map(
        on_device,
        mesh=mesh,
        in_specs=(
            P(("grp", "section"), None),
            P(("grp", "section"), None),
            P(),
            P(),
            P(),
            P(),
            P(),
            P(),
            P(),
            P("section", None, None),
            P("section", None, None),
            P("section", "grp", None),
            P(),
            P(),
            P(),
        ),
        out_specs=P(("grp", "section"), None),
        check_vma=False,
    )
```

profile of v0, /device:TPU:0, one launch (start us, length us, event | category | flops | bytes accessed | tf_op | source)
XLA Modules:
  0.0 692.2 jit_solution(14145736935525604301)
XLA Ops:
  8.5 23.6 %all_gather.6 = bf16[768,64]{1,0:T(8,128)(2,1)S(1)} all-gather(bf16[48,64]{1,0:T(8,128)(2,1)S(1)} %copy-done.7), channel_id=1, replica_groups=mesh['grp'=2,'section'=16] {'section'}, dimensions={0}, use_global_device_ids=true | all-gather | bytes 104448 | tf_op jit(solution)/shard_map/all_gather | solution.py:134
  32.1 17.9 %all_gather.7 = bf16[768,64]{1,0:T(8,128)(2,1)S(1)} all-gather(bf16[48,64]{1,0:T(8,128)(2,1)S(1)} %copy-done.8), channel_id=1, replica_groups=mesh['grp'=2,'section'=16] {'section'}, dimensions={0}, use_global_device_ids=true | all-gather | bytes 104448 | tf_op jit(solution)/shard_map/all_gather | solution.py:135
  54.7 562.6 %while.25 = (s32[]{:T(128)}, bf16[32,3072]{1,0:T(8,128)(2,1)}, bf16[32,3072]{1,0:T(8,128)(2,1)S(1)}, bf16[1024,768]{0,1:T(8,128)(2,1)}, f32[1024,64]{1,0:T(8,128...) while((s32[]{:T(128)}, bf16[32,3072]{1,0:T(8,128)(2,1)}, ...), condition=%wide.region_12.13_spmd, body=%wide.region_1.12_spmd.sunk | while | flops 2714486016 | bytes 100601624 | solution.py:245
  62.3 9.7 %collective-permute-done.1 = bf16[64,3072]{1,0:T(8,128)(2,1)S(1)} collective-permute-done((bf16[64,3072]{1,0:T(8,128)(2,1)S(1)}, bf16[64,3072]{1,0:T(8,128)(2,1)S(1)}, u32[]{:S(2)}, u32[]{:S(2)}) %collective-permute-start.1) | collective-permute-done | bytes 393248 | tf_op jit(solution)/shard_map/while/body/eval_jaxpr/ppermute | solution.py:23
  73.1 18.2 %collective-permute-done.2 = bf16[128,3072]{1,0:T(8,128)(2,1)} collective-permute-done((bf16[128,3072]{1,0:T(8,128)(2,1)S(1)}, bf16[128,3072]{1,0:T(8,128)(2,1)}, u32[]{:S(2)}, u32[]{:S(2)}) %collective-permute-start.2) | collective-permute-done | bytes 786464 | tf_op jit(solution)/shard_map/while/body/eval_jaxpr/ppermute | solution.py:23
  93.3 25.1 %conditional.2 = (bf16[1024,768]{0,1:T(8,128)(2,1)}, bf16[128,3072]{1,0:T(8,128)(2,1)S(1)}, bf16[128,3072]{1,0:T(8,128)(2,1)S(1)}) conditional(s32[]{:T(128)} %convert_element_type.288, bf16[1024,768]{0,1:T(8,128)(2,1)} %get-tuple-element.1047, (s32[]{:T(128)}, pred[]{:T(512)}, bf16[256,3072]{1,0:T(8,128)(2,1)S(1)}, bf16[256,3072]{1,0:T(8,128)(2,1)S(1)}, ...), branch_computations={%region_2.2_spmd, %region_3.9_spmd} | conditional | flops 2658447616 | bytes 57946768 | solution.py:214
  95.2 6.2 fusion.7
  113.6 3.5 fusion.16
  118.9 17.8 %collective-permute-done.3 = bf16[128,3072]{1,0:T(8,128)(2,1)S(1)} collective-permute-done((bf16[128,3072]{1,0:T(8,128)(2,1)S(1)}, bf16[128,3072]{1,0:T(8,128)(2,1)S(1)}, u32[]{:S(2)}, u32[]{:S(2)}) %collective-permute-start.3) | collective-permute-done | bytes 786464 | tf_op jit(solution)/shard_map/while/body/eval_jaxpr/ppermute | solution.py:23
  138.8 7.1 %collective-permute-done.4 = bf16[64,3072]{1,0:T(8,128)(2,1)S(1)} collective-permute-done((bf16[64,3072]{1,0:T(8,128)(2,1)S(1)}, bf16[64,3072]{1,0:T(8,128)(2,1)S(1)}, u32[]{:S(2)}, u32[]{:S(2)}) %collective-permute-start.4) | collective-permute-done | bytes 393248 | tf_op jit(solution)/shard_map/while/body/eval_jaxpr/ppermute | solution.py:23
  154.5 3.7 collective-permute-done.7
  165.9 9.5 %collective-permute-done.1 = bf16[64,3072]{1,0:T(8,128)(2,1)S(1)} collective-permute-done((bf16[64,3072]{1,0:T(8,128)(2,1)S(1)}, bf16[64,3072]{1,0:T(8,128)(2,1)S(1)}, u32[]{:S(2)}, u32[]{:S(2)}) %collective-permute-start.1) | collective-permute-done | bytes 393248 | tf_op jit(solution)/shard_map/while/body/eval_jaxpr/ppermute | solution.py:23
  175.5 9.3 %collective-permute-start.2 = (bf16[128,3072]{1,0:T(8,128)(2,1)S(1)}, bf16[128,3072]{1,0:T(8,128)(2,1)}, u32[]{:S(2)}, u32[]{:S(2)}) collective-permute-start(bf16[128,3072]{1,0:T(8,128)(2,1)S(1)} %maximum_select_fusion.6), channel_id=1, source_target_pairs={{0,4},{1,5},{2,6},{3,7},{4,0},{5,1},{6,2},{7,3},{8,12},{9,13},{10,... | collective-permute-start | bytes 2359304 | tf_op jit(solution)/shard_map/while/body/eval_jaxpr/ppermute | solution.py:23
  185.4 16.4 %collective-permute-done.2 = bf16[128,3072]{1,0:T(8,128)(2,1)} collective-permute-done((bf16[128,3072]{1,0:T(8,128)(2,1)S(1)}, bf16[128,3072]{1,0:T(8,128)(2,1)}, u32[]{:S(2)}, u32[]{:S(2)}) %collective-permute-start.2) | collective-permute-done | bytes 786464 | tf_op jit(solution)/shard_map/while/body/eval_jaxpr/ppermute | solution.py:23
  203.9 25.1 %conditional.2 = (bf16[1024,768]{0,1:T(8,128)(2,1)}, bf16[128,3072]{1,0:T(8,128)(2,1)S(1)}, bf16[128,3072]{1,0:T(8,128)(2,1)S(1)}) conditional(s32[]{:T(128)} %convert_element_type.288, bf16[1024,768]{0,1:T(8,128)(2,1)} %get-tuple-element.1047, (s32[]{:T(128)}, pred[]{:T(512)}, bf16[256,3072]{1,0:T(8,128)(2,1)S(1)}, bf16[256,3072]{1,0:T(8,128)(2,1)S(1)}, ...), branch_computations={%region_2.2_spmd, %region_3.9_spmd} | conditional | flops 2658447616 | bytes 57946768 | solution.py:214
  205.8 6.2 fusion.7
  224.2 3.5 fusion.16
  231.0 16.4 %collective-permute-done.3 = bf16[128,3072]{1,0:T(8,128)(2,1)S(1)} collective-permute-done((bf16[128,3072]{1,0:T(8,128)(2,1)S(1)}, bf16[128,3072]{1,0:T(8,128)(2,1)S(1)}, u32[]{:S(2)}, u32[]{:S(2)}) %collective-permute-start.3) | collective-permute-done | bytes 786464 | tf_op jit(solution)/shard_map/while/body/eval_jaxpr/ppermute | solution.py:23
  249.5 7.2 %collective-permute-done.4 = bf16[64,3072]{1,0:T(8,128)(2,1)S(1)} collective-permute-done((bf16[64,3072]{1,0:T(8,128)(2,1)S(1)}, bf16[64,3072]{1,0:T(8,128)(2,1)S(1)}, u32[]{:S(2)}, u32[]{:S(2)}) %collective-permute-start.4) | collective-permute-done | bytes 393248 | tf_op jit(solution)/shard_map/while/body/eval_jaxpr/ppermute | solution.py:23
  258.7 6.0 collective-permute-start.6
  269.3 3.4 collective-permute-done.7
  280.4 9.5 %collective-permute-done.1 = bf16[64,3072]{1,0:T(8,128)(2,1)S(1)} collective-permute-done((bf16[64,3072]{1,0:T(8,128)(2,1)S(1)}, bf16[64,3072]{1,0:T(8,128)(2,1)S(1)}, u32[]{:S(2)}, u32[]{:S(2)}) %collective-permute-start.1) | collective-permute-done | bytes 393248 | tf_op jit(solution)/shard_map/while/body/eval_jaxpr/ppermute | solution.py:23
  290.0 9.6 %collective-permute-start.2 = (bf16[128,3072]{1,0:T(8,128)(2,1)S(1)}, bf16[128,3072]{1,0:T(8,128)(2,1)}, u32[]{:S(2)}, u32[]{:S(2)}) collective-permute-start(bf16[128,3072]{1,0:T(8,128)(2,1)S(1)} %maximum_select_fusion.6), channel_id=1, source_target_pairs={{0,4},{1,5},{2,6},{3,7},{4,0},{5,1},{6,2},{7,3},{8,12},{9,13},{10,... | collective-permute-start | bytes 2359304 | tf_op jit(solution)/shard_map/while/body/eval_jaxpr/ppermute | solution.py:23
  300.3 16.4 %collective-permute-done.2 = bf16[128,3072]{1,0:T(8,128)(2,1)} collective-permute-done((bf16[128,3072]{1,0:T(8,128)(2,1)S(1)}, bf16[128,3072]{1,0:T(8,128)(2,1)}, u32[]{:S(2)}, u32[]{:S(2)}) %collective-permute-start.2) | collective-permute-done | bytes 786464 | tf_op jit(solution)/shard_map/while/body/eval_jaxpr/ppermute | solution.py:23
  318.8 25.1 %conditional.2 = (bf16[1024,768]{0,1:T(8,128)(2,1)}, bf16[128,3072]{1,0:T(8,128)(2,1)S(1)}, bf16[128,3072]{1,0:T(8,128)(2,1)S(1)}) conditional(s32[]{:T(128)} %convert_element_type.288, bf16[1024,768]{0,1:T(8,128)(2,1)} %get-tuple-element.1047, (s32[]{:T(128)}, pred[]{:T(512)}, bf16[256,3072]{1,0:T(8,128)(2,1)S(1)}, bf16[256,3072]{1,0:T(8,128)(2,1)S(1)}, ...), branch_computations={%region_2.2_spmd, %region_3.9_spmd} | conditional | flops 2658447616 | bytes 57946768 | solution.py:214
  320.7 6.2 fusion.7
  339.0 3.5 fusion.16
  345.8 16.4 %collective-permute-done.3 = bf16[128,3072]{1,0:T(8,128)(2,1)S(1)} collective-permute-done((bf16[128,3072]{1,0:T(8,128)(2,1)S(1)}, bf16[128,3072]{1,0:T(8,128)(2,1)S(1)}, u32[]{:S(2)}, u32[]{:S(2)}) %collective-permute-start.3) | collective-permute-done | bytes 786464 | tf_op jit(solution)/shard_map/while/body/eval_jaxpr/ppermute | solution.py:23
  364.4 7.2 %collective-permute-done.4 = bf16[64,3072]{1,0:T(8,128)(2,1)S(1)} collective-permute-done((bf16[64,3072]{1,0:T(8,128)(2,1)S(1)}, bf16[64,3072]{1,0:T(8,128)(2,1)S(1)}, u32[]{:S(2)}, u32[]{:S(2)}) %collective-permute-start.4) | collective-permute-done | bytes 393248 | tf_op jit(solution)/shard_map/while/body/eval_jaxpr/ppermute | solution.py:23
  373.5 6.0 collective-permute-start.6
  384.2 3.4 collective-permute-done.7
  395.2 9.5 %collective-permute-done.1 = bf16[64,3072]{1,0:T(8,128)(2,1)S(1)} collective-permute-done((bf16[64,3072]{1,0:T(8,128)(2,1)S(1)}, bf16[64,3072]{1,0:T(8,128)(2,1)S(1)}, u32[]{:S(2)}, u32[]{:S(2)}) %collective-permute-start.1) | collective-permute-done | bytes 393248 | tf_op jit(solution)/shard_map/while/body/eval_jaxpr/ppermute | solution.py:23
  404.9 9.6 %collective-permute-start.2 = (bf16[128,3072]{1,0:T(8,128)(2,1)S(1)}, bf16[128,3072]{1,0:T(8,128)(2,1)}, u32[]{:S(2)}, u32[]{:S(2)}) collective-permute-start(bf16[128,3072]{1,0:T(8,128)(2,1)S(1)} %maximum_select_fusion.6), channel_id=1, source_target_pairs={{0,4},{1,5},{2,6},{3,7},{4,0},{5,1},{6,2},{7,3},{8,12},{9,13},{10,... | collective-permute-start | bytes 2359304 | tf_op jit(solution)/shard_map/while/body/eval_jaxpr/ppermute | solution.py:23
  415.1 16.4 %collective-permute-done.2 = bf16[128,3072]{1,0:T(8,128)(2,1)} collective-permute-done((bf16[128,3072]{1,0:T(8,128)(2,1)S(1)}, bf16[128,3072]{1,0:T(8,128)(2,1)}, u32[]{:S(2)}, u32[]{:S(2)}) %collective-permute-start.2) | collective-permute-done | bytes 786464 | tf_op jit(solution)/shard_map/while/body/eval_jaxpr/ppermute | solution.py:23
  433.6 25.1 %conditional.2 = (bf16[1024,768]{0,1:T(8,128)(2,1)}, bf16[128,3072]{1,0:T(8,128)(2,1)S(1)}, bf16[128,3072]{1,0:T(8,128)(2,1)S(1)}) conditional(s32[]{:T(128)} %convert_element_type.288, bf16[1024,768]{0,1:T(8,128)(2,1)} %get-tuple-element.1047, (s32[]{:T(128)}, pred[]{:T(512)}, bf16[256,3072]{1,0:T(8,128)(2,1)S(1)}, bf16[256,3072]{1,0:T(8,128)(2,1)S(1)}, ...), branch_computations={%region_2.2_spmd, %region_3.9_spmd} | conditional | flops 2658447616 | bytes 57946768 | solution.py:214
  435.5 6.2 fusion.7
  453.9 3.5 fusion.16
  460.7 16.4 %collective-permute-done.3 = bf16[128,3072]{1,0:T(8,128)(2,1)S(1)} collective-permute-done((bf16[128,3072]{1,0:T(8,128)(2,1)S(1)}, bf16[128,3072]{1,0:T(8,128)(2,1)S(1)}, u32[]{:S(2)}, u32[]{:S(2)}) %collective-permute-start.3) | collective-permute-done | bytes 786464 | tf_op jit(solution)/shard_map/while/body/eval_jaxpr/ppermute | solution.py:23
  479.2 7.2 %collective-permute-done.4 = bf16[64,3072]{1,0:T(8,128)(2,1)S(1)} collective-permute-done((bf16[64,3072]{1,0:T(8,128)(2,1)S(1)}, bf16[64,3072]{1,0:T(8,128)(2,1)S(1)}, u32[]{:S(2)}, u32[]{:S(2)}) %collective-permute-start.4) | collective-permute-done | bytes 393248 | tf_op jit(solution)/shard_map/while/body/eval_jaxpr/ppermute | solution.py:23
  488.4 6.0 collective-permute-start.6
  499.0 3.4 collective-permute-done.7
  510.1 9.5 %collective-permute-done.1 = bf16[64,3072]{1,0:T(8,128)(2,1)S(1)} collective-permute-done((bf16[64,3072]{1,0:T(8,128)(2,1)S(1)}, bf16[64,3072]{1,0:T(8,128)(2,1)S(1)}, u32[]{:S(2)}, u32[]{:S(2)}) %collective-permute-start.1) | collective-permute-done | bytes 393248 | tf_op jit(solution)/shard_map/while/body/eval_jaxpr/ppermute | solution.py:23
  519.7 9.6 %collective-permute-start.2 = (bf16[128,3072]{1,0:T(8,128)(2,1)S(1)}, bf16[128,3072]{1,0:T(8,128)(2,1)}, u32[]{:S(2)}, u32[]{:S(2)}) collective-permute-start(bf16[128,3072]{1,0:T(8,128)(2,1)S(1)} %maximum_select_fusion.6), channel_id=1, source_target_pairs={{0,4},{1,5},{2,6},{3,7},{4,0},{5,1},{6,2},{7,3},{8,12},{9,13},{10,... | collective-permute-start | bytes 2359304 | tf_op jit(solution)/shard_map/while/body/eval_jaxpr/ppermute | solution.py:23
  530.0 16.4 %collective-permute-done.2 = bf16[128,3072]{1,0:T(8,128)(2,1)} collective-permute-done((bf16[128,3072]{1,0:T(8,128)(2,1)S(1)}, bf16[128,3072]{1,0:T(8,128)(2,1)}, u32[]{:S(2)}, u32[]{:S(2)}) %collective-permute-start.2) | collective-permute-done | bytes 786464 | tf_op jit(solution)/shard_map/while/body/eval_jaxpr/ppermute | solution.py:23
  550.6 16.4 %collective-permute-done.3 = bf16[128,3072]{1,0:T(8,128)(2,1)S(1)} collective-permute-done((bf16[128,3072]{1,0:T(8,128)(2,1)S(1)}, bf16[128,3072]{1,0:T(8,128)(2,1)S(1)}, u32[]{:S(2)}, u32[]{:S(2)}) %collective-permute-start.3) | collective-permute-done | bytes 786464 | tf_op jit(solution)/shard_map/while/body/eval_jaxpr/ppermute | solution.py:23
  569.1 7.2 %collective-permute-done.4 = bf16[64,3072]{1,0:T(8,128)(2,1)S(1)} collective-permute-done((bf16[64,3072]{1,0:T(8,128)(2,1)S(1)}, bf16[64,3072]{1,0:T(8,128)(2,1)S(1)}, u32[]{:S(2)}, u32[]{:S(2)}) %collective-permute-start.4) | collective-permute-done | bytes 393248 | tf_op jit(solution)/shard_map/while/body/eval_jaxpr/ppermute | solution.py:23
  578.3 31.0 %collective-permute-start.6 = (bf16[32,3072]{1,0:T(8,128)(2,1)S(1)}, bf16[32,3072]{1,0:T(8,128)(2,1)}, u32[]{:S(2)}, u32[]{:S(2)}) collective-permute-start(bf16[32,3072]{1,0:T(8,128)(2,1)S(1)} %get-tuple-element.999), channel_id=1, source_target_pairs={{0,8},{1,9},{2,10},{3,11},{4,12},{5,13},{6,14},{7,15},{16,24},{17,... | collective-permute-start | bytes 589832 | tf_op jit(solution)/shard_map/while/body/eval_jaxpr/ppermute | solution.py:29
  619.1 66.3 %reduce-scatter.2.cloned.1.call-done = f32[48,64]{1,0:T(8,128)} async-done(((f32[768,64]{1,0:T(8,128)}), f32[48,64]{1,0:T(8,128)}) %reduce-scatter.2.cloned.1.call-update) | async-done | bytes 12304 | tf_op jit(solution)/shard_map/reduce_scatter | solution.py:246
  (378 shorter events, 167.1 us)
Async XLA Ops:
  6.5 43.5 %copy-start = (f32[2,3,3072]{2,0,1:T(2,128)S(1)}, f32[2,3,3072]{2,0,1:T(2,128)}, u32[]{:S(2)}) copy-start(f32[2,3,3072]{2,0,1:T(2,128)} %param.26) | copy-start | bytes 221188
  6.5 25.6 %copy-start.8 = (bf16[48,64]{1,0:T(8,128)(2,1)S(1)}, bf16[48,64]{1,0:T(8,128)(2,1)}, u32[]{:S(2)}) copy-start(bf16[48,64]{1,0:T(8,128)(2,1)} %param.20) | copy-start | bytes 18436
  6.5 43.6 %copy-start.10 = (f32[2,2,128]{2,1,0:T(2,128)S(1)}, f32[2,2,128]{2,1,0:T(2,128)}, u32[]{:S(2)}) copy-start(f32[2,2,128]{2,1,0:T(2,128)} %param.27) | copy-start | bytes 6148
  6.5 43.6 %copy-start.9 = (s32[2,6,3]{1,0,2:T(2,128)S(1)}, s32[2,6,3]{1,0,2:T(2,128)}, u32[]{:S(2)}) copy-start(s32[2,6,3]{1,0,2:T(2,128)} %param.22) | copy-start | bytes 436
  6.6 43.7 %copy-start.12 = (s32[2,6]{1,0:T(2,128)S(1)}, s32[2,6]{1,0:T(2,128)}, u32[]{:S(2)}) copy-start(s32[2,6]{1,0:T(2,128)} %param.23) | copy-start | bytes 148
  6.6 678.8 %reduce-scatter.2.cloned.1.call-start = ((), (), s32[]{:S(2)}) async-start(), calls=%async_computation.1 | async-start | bytes 417792 | tf_op jit(solution)/shard_map/reduce_scatter | solution.py:246
  59.1 1.4 collective-permute-start
  60.6 11.4 %collective-permute-start.1 = (bf16[64,3072]{1,0:T(8,128)(2,1)S(1)}, bf16[64,3072]{1,0:T(8,128)(2,1)S(1)}, u32[]{:S(2)}, u32[]{:S(2)}) collective-permute-start(bf16[64,3072]{1,0:T(8,128)(2,1)S(1)} %maximum_select_fusion.5), channel_id=1, source_target_pairs={{0,2},{1,3},{2,0},{3,1},{4,6},{5,7},{6,4},{7,5},{8,10},{9,11},{10,... | collective-permute-start | bytes 1179656 | tf_op jit(solution)/shard_map/while/body/eval_jaxpr/ppermute | solution.py:23
  72.2 19.1 %collective-permute-start.2 = (bf16[128,3072]{1,0:T(8,128)(2,1)S(1)}, bf16[128,3072]{1,0:T(8,128)(2,1)}, u32[]{:S(2)}, u32[]{:S(2)}) collective-permute-start(bf16[128,3072]{1,0:T(8,128)(2,1)S(1)} %maximum_select_fusion.6), channel_id=1, source_target_pairs={{0,4},{1,5},{2,6},{3,7},{4,0},{5,1},{6,2},{7,3},{8,12},{9,13},{10,... | collective-permute-start | bytes 2359304 | tf_op jit(solution)/shard_map/while/body/eval_jaxpr/ppermute | solution.py:23
  118.6 18.1 %collective-permute-start.3 = (bf16[128,3072]{1,0:T(8,128)(2,1)S(1)}, bf16[128,3072]{1,0:T(8,128)(2,1)S(1)}, u32[]{:S(2)}, u32[]{:S(2)}) collective-permute-start(bf16[128,3072]{1,0:T(8,128)(2,1)S(1)} %broadcast_select_fusion.7), channel_id=1, source_target_pairs={{0,4},{1,5},{2,6},{3,7},{4,0},{5,1},{6,2},{7,3},{8,12},{9,13},{10,... | collective-permute-start | bytes 2359304 | tf_op jit(solution)/shard_map/while/body/eval_jaxpr/ppermute | solution.py:23
  137.1 8.9 %collective-permute-start.4 = (bf16[64,3072]{1,0:T(8,128)(2,1)S(1)}, bf16[64,3072]{1,0:T(8,128)(2,1)S(1)}, u32[]{:S(2)}, u32[]{:S(2)}) collective-permute-start(bf16[64,3072]{1,0:T(8,128)(2,1)S(1)} %select_convert_fusion.4), channel_id=1, source_target_pairs={{0,2},{1,3},{2,0},{3,1},{4,6},{5,7},{6,4},{7,5},{8,10},{9,11},{10,... | collective-permute-start | bytes 1179656 | tf_op jit(solution)/shard_map/while/body/eval_jaxpr/ppermute | solution.py:23
  146.1 1.5 collective-permute-start.5
  147.9 6.6 collective-permute-start.6
  150.0 8.2 %collective-permute-start.7 = (bf16[32,3072]{1,0:T(8,128)(2,1)S(1)}, bf16[32,3072]{1,0:T(8,128)(2,1)S(1)}, u32[]{:S(2)}, u32[]{:S(2)}) collective-permute-start(bf16[32,3072]{1,0:T(8,128)(2,1)S(1)} %convert_select_fusion.4), channel_id=1, source_target_pairs={{0,8},{1,9},{2,10},{3,11},{4,12},{5,13},{6,14},{7,15},{16,24},{17,... | collective-permute-start | bytes 589832 | tf_op jit(solution)/shard_map/while/body/eval_jaxpr/ppermute | solution.py:29
  162.6 1.4 collective-permute-start
  164.1 11.2 %collective-permute-start.1 = (bf16[64,3072]{1,0:T(8,128)(2,1)S(1)}, bf16[64,3072]{1,0:T(8,128)(2,1)S(1)}, u32[]{:S(2)}, u32[]{:S(2)}) collective-permute-start(bf16[64,3072]{1,0:T(8,128)(2,1)S(1)} %maximum_select_fusion.5), channel_id=1, source_target_pairs={{0,2},{1,3},{2,0},{3,1},{4,6},{5,7},{6,4},{7,5},{8,10},{9,11},{10,... | collective-permute-start | bytes 1179656 | tf_op jit(solution)/shard_map/while/body/eval_jaxpr/ppermute | solution.py:23
  175.5 26.4 %collective-permute-start.2 = (bf16[128,3072]{1,0:T(8,128)(2,1)S(1)}, bf16[128,3072]{1,0:T(8,128)(2,1)}, u32[]{:S(2)}, u32[]{:S(2)}) collective-permute-start(bf16[128,3072]{1,0:T(8,128)(2,1)S(1)} %maximum_select_fusion.6), channel_id=1, source_target_pairs={{0,4},{1,5},{2,6},{3,7},{4,0},{5,1},{6,2},{7,3},{8,12},{9,13},{10,... | collective-permute-start | bytes 2359304 | tf_op jit(solution)/shard_map/while/body/eval_jaxpr/ppermute | solution.py:23
  229.2 18.2 %collective-permute-start.3 = (bf16[128,3072]{1,0:T(8,128)(2,1)S(1)}, bf16[128,3072]{1,0:T(8,128)(2,1)S(1)}, u32[]{:S(2)}, u32[]{:S(2)}) collective-permute-start(bf16[128,3072]{1,0:T(8,128)(2,1)S(1)} %broadcast_select_fusion.7), channel_id=1, source_target_pairs={{0,4},{1,5},{2,6},{3,7},{4,0},{5,1},{6,2},{7,3},{8,12},{9,13},{10,... | collective-permute-start | bytes 2359304 | tf_op jit(solution)/shard_map/while/body/eval_jaxpr/ppermute | solution.py:23
  247.8 10.6 %copy-start.3 = (bf16[32,3072]{1,0:T(8,128)(2,1)S(1)}, bf16[32,3072]{1,0:T(8,128)(2,1)}, u32[]{:S(2)}) copy-start(bf16[32,3072]{1,0:T(8,128)(2,1)} %get-tuple-element.993) | copy-start | bytes 589828 | tf_op jit(solution)/shard_map/while
  247.8 8.9 %collective-permute-start.4 = (bf16[64,3072]{1,0:T(8,128)(2,1)S(1)}, bf16[64,3072]{1,0:T(8,128)(2,1)S(1)}, u32[]{:S(2)}, u32[]{:S(2)}) collective-permute-start(bf16[64,3072]{1,0:T(8,128)(2,1)S(1)} %select_convert_fusion.4), channel_id=1, source_target_pairs={{0,2},{1,3},{2,0},{3,1},{4,6},{5,7},{6,4},{7,5},{8,10},{9,11},{10,... | collective-permute-start | bytes 1179656 | tf_op jit(solution)/shard_map/while/body/eval_jaxpr/ppermute | solution.py:23
  256.9 1.5 collective-permute-start.5
  258.7 10.7 %collective-permute-start.6 = (bf16[32,3072]{1,0:T(8,128)(2,1)S(1)}, bf16[32,3072]{1,0:T(8,128)(2,1)}, u32[]{:S(2)}, u32[]{:S(2)}) collective-permute-start(bf16[32,3072]{1,0:T(8,128)(2,1)S(1)} %get-tuple-element.999), channel_id=1, source_target_pairs={{0,8},{1,9},{2,10},{3,11},{4,12},{5,13},{6,14},{7,15},{16,24},{17,... | collective-permute-start | bytes 589832 | tf_op jit(solution)/shard_map/while/body/eval_jaxpr/ppermute | solution.py:29
  264.8 7.9 %collective-permute-start.7 = (bf16[32,3072]{1,0:T(8,128)(2,1)S(1)}, bf16[32,3072]{1,0:T(8,128)(2,1)S(1)}, u32[]{:S(2)}, u32[]{:S(2)}) collective-permute-start(bf16[32,3072]{1,0:T(8,128)(2,1)S(1)} %convert_select_fusion.4), channel_id=1, source_target_pairs={{0,8},{1,9},{2,10},{3,11},{4,12},{5,13},{6,14},{7,15},{16,24},{17,... | collective-permute-start | bytes 589832 | tf_op jit(solution)/shard_map/while/body/eval_jaxpr/ppermute | solution.py:29
  277.1 1.4 collective-permute-start
  278.6 11.2 %collective-permute-start.1 = (bf16[64,3072]{1,0:T(8,128)(2,1)S(1)}, bf16[64,3072]{1,0:T(8,128)(2,1)S(1)}, u32[]{:S(2)}, u32[]{:S(2)}) collective-permute-start(bf16[64,3072]{1,0:T(8,128)(2,1)S(1)} %maximum_select_fusion.5), channel_id=1, source_target_pairs={{0,2},{1,3},{2,0},{3,1},{4,6},{5,7},{6,4},{7,5},{8,10},{9,11},{10,... | collective-permute-start | bytes 1179656 | tf_op jit(solution)/shard_map/while/body/eval_jaxpr/ppermute | solution.py:23
  290.0 26.7 %collective-permute-start.2 = (bf16[128,3072]{1,0:T(8,128)(2,1)S(1)}, bf16[128,3072]{1,0:T(8,128)(2,1)}, u32[]{:S(2)}, u32[]{:S(2)}) collective-permute-start(bf16[128,3072]{1,0:T(8,128)(2,1)S(1)} %maximum_select_fusion.6), channel_id=1, source_target_pairs={{0,4},{1,5},{2,6},{3,7},{4,0},{5,1},{6,2},{7,3},{8,12},{9,13},{10,... | collective-permute-start | bytes 2359304 | tf_op jit(solution)/shard_map/while/body/eval_jaxpr/ppermute | solution.py:23
  344.0 18.2 %collective-permute-start.3 = (bf16[128,3072]{1,0:T(8,128)(2,1)S(1)}, bf16[128,3072]{1,0:T(8,128)(2,1)S(1)}, u32[]{:S(2)}, u32[]{:S(2)}) collective-permute-start(bf16[128,3072]{1,0:T(8,128)(2,1)S(1)} %broadcast_select_fusion.7), channel_id=1, source_target_pairs={{0,4},{1,5},{2,6},{3,7},{4,0},{5,1},{6,2},{7,3},{8,12},{9,13},{10,... | collective-permute-start | bytes 2359304 | tf_op jit(solution)/shard_map/while/body/eval_jaxpr/ppermute | solution.py:23
  362.6 8.9 %collective-permute-start.4 = (bf16[64,3072]{1,0:T(8,128)(2,1)S(1)}, bf16[64,3072]{1,0:T(8,128)(2,1)S(1)}, u32[]{:S(2)}, u32[]{:S(2)}) collective-permute-start(bf16[64,3072]{1,0:T(8,128)(2,1)S(1)} %select_convert_fusion.4), channel_id=1, source_target_pairs={{0,2},{1,3},{2,0},{3,1},{4,6},{5,7},{6,4},{7,5},{8,10},{9,11},{10,... | collective-permute-start | bytes 1179656 | tf_op jit(solution)/shard_map/while/body/eval_jaxpr/ppermute | solution.py:23
  371.7 1.5 collective-permute-start.5
  373.5 10.6 %collective-permute-start.6 = (bf16[32,3072]{1,0:T(8,128)(2,1)S(1)}, bf16[32,3072]{1,0:T(8,128)(2,1)}, u32[]{:S(2)}, u32[]{:S(2)}) collective-permute-start(bf16[32,3072]{1,0:T(8,128)(2,1)S(1)} %get-tuple-element.999), channel_id=1, source_target_pairs={{0,8},{1,9},{2,10},{3,11},{4,12},{5,13},{6,14},{7,15},{16,24},{17,... | collective-permute-start | bytes 589832 | tf_op jit(solution)/shard_map/while/body/eval_jaxpr/ppermute | solution.py:29
  379.7 7.9 %collective-permute-start.7 = (bf16[32,3072]{1,0:T(8,128)(2,1)S(1)}, bf16[32,3072]{1,0:T(8,128)(2,1)S(1)}, u32[]{:S(2)}, u32[]{:S(2)}) collective-permute-start(bf16[32,3072]{1,0:T(8,128)(2,1)S(1)} %convert_select_fusion.4), channel_id=1, source_target_pairs={{0,8},{1,9},{2,10},{3,11},{4,12},{5,13},{6,14},{7,15},{16,24},{17,... | collective-permute-start | bytes 589832 | tf_op jit(solution)/shard_map/while/body/eval_jaxpr/ppermute | solution.py:29
  391.9 1.4 collective-permute-start
  393.5 11.2 %collective-permute-start.1 = (bf16[64,3072]{1,0:T(8,128)(2,1)S(1)}, bf16[64,3072]{1,0:T(8,128)(2,1)S(1)}, u32[]{:S(2)}, u32[]{:S(2)}) collective-permute-start(bf16[64,3072]{1,0:T(8,128)(2,1)S(1)} %maximum_select_fusion.5), channel_id=1, source_target_pairs={{0,2},{1,3},{2,0},{3,1},{4,6},{5,7},{6,4},{7,5},{8,10},{9,11},{10,... | collective-permute-start | bytes 1179656 | tf_op jit(solution)/shard_map/while/body/eval_jaxpr/ppermute | solution.py:23
  404.9 26.7 %collective-permute-start.2 = (bf16[128,3072]{1,0:T(8,128)(2,1)S(1)}, bf16[128,3072]{1,0:T(8,128)(2,1)}, u32[]{:S(2)}, u32[]{:S(2)}) collective-permute-start(bf16[128,3072]{1,0:T(8,128)(2,1)S(1)} %maximum_select_fusion.6), channel_id=1, source_target_pairs={{0,4},{1,5},{2,6},{3,7},{4,0},{5,1},{6,2},{7,3},{8,12},{9,13},{10,... | collective-permute-start | bytes 2359304 | tf_op jit(solution)/shard_map/while/body/eval_jaxpr/ppermute | solution.py:23
  458.9 18.2 %collective-permute-start.3 = (bf16[128,3072]{1,0:T(8,128)(2,1)S(1)}, bf16[128,3072]{1,0:T(8,128)(2,1)S(1)}, u32[]{:S(2)}, u32[]{:S(2)}) collective-permute-start(bf16[128,3072]{1,0:T(8,128)(2,1)S(1)} %broadcast_select_fusion.7), channel_id=1, source_target_pairs={{0,4},{1,5},{2,6},{3,7},{4,0},{5,1},{6,2},{7,3},{8,12},{9,13},{10,... | collective-permute-start | bytes 2359304 | tf_op jit(solution)/shard_map/while/body/eval_jaxpr/ppermute | solution.py:23
  477.5 8.9 %collective-permute-start.4 = (bf16[64,3072]{1,0:T(8,128)(2,1)S(1)}, bf16[64,3072]{1,0:T(8,128)(2,1)S(1)}, u32[]{:S(2)}, u32[]{:S(2)}) collective-permute-start(bf16[64,3072]{1,0:T(8,128)(2,1)S(1)} %select_convert_fusion.4), channel_id=1, source_target_pairs={{0,2},{1,3},{2,0},{3,1},{4,6},{5,7},{6,4},{7,5},{8,10},{9,11},{10,... | collective-permute-start | bytes 1179656 | tf_op jit(solution)/shard_map/while/body/eval_jaxpr/ppermute | solution.py:23
  486.6 1.5 collective-permute-start.5
  488.4 10.6 %collective-permute-start.6 = (bf16[32,3072]{1,0:T(8,128)(2,1)S(1)}, bf16[32,3072]{1,0:T(8,128)(2,1)}, u32[]{:S(2)}, u32[]{:S(2)}) collective-permute-start(bf16[32,3072]{1,0:T(8,128)(2,1)S(1)} %get-tuple-element.999), channel_id=1, source_target_pairs={{0,8},{1,9},{2,10},{3,11},{4,12},{5,13},{6,14},{7,15},{16,24},{17,... | collective-permute-start | bytes 589832 | tf_op jit(solution)/shard_map/while/body/eval_jaxpr/ppermute | solution.py:29
  494.5 7.9 %collective-permute-start.7 = (bf16[32,3072]{1,0:T(8,128)(2,1)S(1)}, bf16[32,3072]{1,0:T(8,128)(2,1)S(1)}, u32[]{:S(2)}, u32[]{:S(2)}) collective-permute-start(bf16[32,3072]{1,0:T(8,128)(2,1)S(1)} %convert_select_fusion.4), channel_id=1, source_target_pairs={{0,8},{1,9},{2,10},{3,11},{4,12},{5,13},{6,14},{7,15},{16,24},{17,... | collective-permute-start | bytes 589832 | tf_op jit(solution)/shard_map/while/body/eval_jaxpr/ppermute | solution.py:29
  506.8 1.4 collective-permute-start
  508.3 11.2 %collective-permute-start.1 = (bf16[64,3072]{1,0:T(8,128)(2,1)S(1)}, bf16[64,3072]{1,0:T(8,128)(2,1)S(1)}, u32[]{:S(2)}, u32[]{:S(2)}) collective-permute-start(bf16[64,3072]{1,0:T(8,128)(2,1)S(1)} %maximum_select_fusion.5), channel_id=1, source_target_pairs={{0,2},{1,3},{2,0},{3,1},{4,6},{5,7},{6,4},{7,5},{8,10},{9,11},{10,... | collective-permute-start | bytes 1179656 | tf_op jit(solution)/shard_map/while/body/eval_jaxpr/ppermute | solution.py:23
  519.7 26.7 %collective-permute-start.2 = (bf16[128,3072]{1,0:T(8,128)(2,1)S(1)}, bf16[128,3072]{1,0:T(8,128)(2,1)}, u32[]{:S(2)}, u32[]{:S(2)}) collective-permute-start(bf16[128,3072]{1,0:T(8,128)(2,1)S(1)} %maximum_select_fusion.6), channel_id=1, source_target_pairs={{0,4},{1,5},{2,6},{3,7},{4,0},{5,1},{6,2},{7,3},{8,12},{9,13},{10,... | collective-permute-start | bytes 2359304 | tf_op jit(solution)/shard_map/while/body/eval_jaxpr/ppermute | solution.py:23
  548.8 18.2 %collective-permute-start.3 = (bf16[128,3072]{1,0:T(8,128)(2,1)S(1)}, bf16[128,3072]{1,0:T(8,128)(2,1)S(1)}, u32[]{:S(2)}, u32[]{:S(2)}) collective-permute-start(bf16[128,3072]{1,0:T(8,128)(2,1)S(1)} %broadcast_select_fusion.7), channel_id=1, source_target_pairs={{0,4},{1,5},{2,6},{3,7},{4,0},{5,1},{6,2},{7,3},{8,12},{9,13},{10,... | collective-permute-start | bytes 2359304 | tf_op jit(solution)/shard_map/while/body/eval_jaxpr/ppermute | solution.py:23
  567.4 8.9 %collective-permute-start.4 = (bf16[64,3072]{1,0:T(8,128)(2,1)S(1)}, bf16[64,3072]{1,0:T(8,128)(2,1)S(1)}, u32[]{:S(2)}, u32[]{:S(2)}) collective-permute-start(bf16[64,3072]{1,0:T(8,128)(2,1)S(1)} %select_convert_fusion.4), channel_id=1, source_target_pairs={{0,2},{1,3},{2,0},{3,1},{4,6},{5,7},{6,4},{7,5},{8,10},{9,11},{10,... | collective-permute-start | bytes 1179656 | tf_op jit(solution)/shard_map/while/body/eval_jaxpr/ppermute | solution.py:23
  576.5 1.5 collective-permute-start.5
  578.0 32.9 %copy-start.11 = (bf16[3072,64]{0,1:T(8,128)(2,1)S(1)}, bf16[3072,64]{0,1:T(8,128)(2,1)}, u32[]{:S(2)}) copy-start(bf16[3072,64]{0,1:T(8,128)(2,1)} %get-tuple-element.1105) | copy-start | bytes 1179652 | tf_op jit(solution)/shard_map/while
  578.3 35.6 %collective-permute-start.6 = (bf16[32,3072]{1,0:T(8,128)(2,1)S(1)}, bf16[32,3072]{1,0:T(8,128)(2,1)}, u32[]{:S(2)}, u32[]{:S(2)}) collective-permute-start(bf16[32,3072]{1,0:T(8,128)(2,1)S(1)} %get-tuple-element.999), channel_id=1, source_target_pairs={{0,8},{1,9},{2,10},{3,11},{4,12},{5,13},{6,14},{7,15},{16,24},{17,... | collective-permute-start | bytes 589832 | tf_op jit(solution)/shard_map/while/body/eval_jaxpr/ppermute | solution.py:29
  609.4 7.9 %collective-permute-start.7 = (bf16[32,3072]{1,0:T(8,128)(2,1)S(1)}, bf16[32,3072]{1,0:T(8,128)(2,1)S(1)}, u32[]{:S(2)}, u32[]{:S(2)}) collective-permute-start(bf16[32,3072]{1,0:T(8,128)(2,1)S(1)} %convert_select_fusion.4), channel_id=1, source_target_pairs={{0,8},{1,9},{2,10},{3,11},{4,12},{5,13},{6,14},{7,15},{16,24},{17,... | collective-permute-start | bytes 589832 | tf_op jit(solution)/shard_map/while/body/eval_jaxpr/ppermute | solution.py:29
  (25 other events, 140.7 us)
Sparse Core Ops, SparseCore 0:
  619.2 66.1 reduce-scatter.1
where the time goes:
time: 694 us; the launch traced here: 692 us
  waiting for transfers between devices  351 us (51%)
  starting transfers between devices  121 us (17%)
  matrix products  75.3 us (11%)
  blocking collectives  41.6 us (6%)
  local copies, waits for them, and re-layouts  38.4 us (6%)
  other arithmetic  37.4 us (5%)
  between operations  13.5 us (2%)
  loops' own time  13 us (2%)
    ppermute x30, waiting for transfers between devices, from_partner(): lax.ppermute(value, axis, [(i, i ^ 1 << distance) for i in range(lax.axis...  261 us
    reduce_scatter x1, waiting for transfers between devices, on_device(): lax.psum_scatter(finished[3][:seq_rows], 'section', scatter_dimension=0,...  66.3 us
    ppermute x30, starting transfers between devices, from_partner(): lax.ppermute(value, axis, [(i, i ^ 1 << distance) for i in range(lax.axis...  64 us
    ppermute x10, starting transfers between devices, from_behind(): lax.ppermute(value, axis, [(source, source + steps) for source in range(l...  57.5 us
    dot_general x4, matrix products, attend_group(): jnp.dot(modded, w_qkv, preferred_element_type=jnp.float32)  24.9 us
    ppermute x10, waiting for transfers between devices, from_behind(): lax.ppermute(value, axis, [(source, source + steps) for source in range(l...  23.7 us
    all_gather x1, blocking collectives, on_device(): lax.all_gather(latent, 'section', axis=0, tiled=True)  23.6 us
    all_gather x1, blocking collectives, on_device(): lax.all_gather(control_latent, 'section', axis=0, tiled=True)  17.9 us
  transfers between devices with their start and end apart: 41, of which 41 were waited for; matrix products, arithmetic and copies ran while one was open for 2% of the time, Pallas kernels for 0%

commit v1 on v0

v1 whole, which is shorter than its diff:
```python
import math

import jax
import jax.numpy as jnp
from jax import lax
from jax.sharding import PartitionSpec as P

HD = 128
HG = 8
TILE = 128

EPSILON = 1e-06


def from_partner(value, axis, distance):
    return lax.ppermute(value, axis, [(i, i ^ 1 << distance) for i in range(lax.axis_size(axis))])


def from_behind(value, axis, steps):
    count = lax.axis_size(axis)
    leading, last = (max(0, -steps), min(count, count - steps))
    return lax.ppermute(value, axis, [(source, source + steps) for source in range(leading, last)])


def modulated(hidden, shift_row, scale_row):
    values = hidden.astype(jnp.float32)
    centered = values - jnp.mean(values, axis=-1, keepdims=True)
    variance = jnp.mean(centered * centered, axis=-1, keepdims=True)
    normed = centered * lax.rsqrt(variance + EPSILON)
    return (normed * (1.0 + scale_row) + shift_row).astype(jnp.bfloat16)


def rms_scaled(values, gain_row):
    return (
        values * lax.rsqrt(jnp.mean(values * values, axis=-1, keepdims=True) + EPSILON) * gain_row
    )


def bit_of(value, bit):
    return (value >> bit) & 1


def block_position(group, bit_order):
    steps = len(bit_order)
    return sum(((group >> b) & 1) << (steps - 1 - k) for k, b in enumerate(bit_order))


def reduce_rows(partial, group_index, bit_order):
    current = partial
    for step, bit in enumerate(bit_order):
        middle = current.shape[0] // 2
        upper = bit_of(group_index, bit)
        kept = lax.dynamic_slice_in_dim(current, upper * middle, middle, 0)
        given = lax.dynamic_slice_in_dim(current, (1 - upper) * middle, middle, 0)
        if step > 0:
            given = given.astype(jnp.bfloat16)
        received = from_partner(given, "section", bit)
        current = kept.astype(jnp.float32) + received.astype(jnp.float32)
    return current


def gather_rows(mine, position, bit_count):
    gathered = mine
    for bit in range(bit_count):
        partner = from_partner(gathered, "section", bit)
        upper = bit_of(position, bit) == 1
        gathered = jnp.where(
            upper,
            jnp.concatenate([partner, gathered]),
            jnp.concatenate([gathered, partner]),
        )
    return gathered


def attend_all(modded, w_qkv, w_out, stale, gain_pair, tile_patch, tile_list, tile_limit, row_order):
    rows = modded.shape[0]
    tiles = rows // TILE
    ksel = tile_list.shape[1]
    head_count = w_out.shape[0] // HD
    projected = jnp.dot(modded, w_qkv, preferred_element_type=jnp.float32).reshape(
        rows, 3, head_count, HD
    )
    queries = rms_scaled(projected[:, 0], gain_pair[0]).astype(jnp.bfloat16)
    keys_new = rms_scaled(projected[:, 1], gain_pair[1]).astype(jnp.bfloat16)
    values_new = projected[:, 2].astype(jnp.bfloat16)
    fresh = jnp.concatenate(
        [keys_new.reshape(rows, head_count * HD), values_new.reshape(rows, head_count * HD)],
        axis=1,
    )
    width = fresh.shape[1]
    memory = jnp.concatenate(
        [fresh.reshape(tiles, TILE, width), stale.reshape(tiles, TILE, width)], axis=0
    )
    use_new = tile_patch[tile_list] <= tile_patch[:, None]
    picked = tile_list + jnp.where(use_new, 0, tiles)
    chosen = memory[picked]
    key_rows = chosen[..., : head_count * HD].reshape(tiles, ksel * TILE, head_count, HD)
    value_rows = chosen[..., head_count * HD :].reshape(tiles, ksel * TILE, head_count, HD)
    query_rows = queries.reshape(tiles, TILE, head_count, HD)
    scores = jnp.einsum(
        "tqhd,tkhd->thqk", query_rows, key_rows, preferred_element_type=jnp.float32
    ) / math.sqrt(HD)
    allowed = (jnp.arange(ksel * TILE) // TILE)[None, :] < tile_limit[:, None]
    scores = jnp.where(allowed[:, None, None, :], scores, -1e30)
    highest = jnp.max(scores, axis=-1, keepdims=True)
    weights = jnp.exp(scores - highest)
    probabilities = (weights / jnp.sum(weights, axis=-1, keepdims=True)).astype(jnp.bfloat16)
    attended = jnp.einsum(
        "thqk,tkhd->tqhd", probabilities, value_rows, preferred_element_type=jnp.float32
    ).astype(jnp.bfloat16)
    attended = attended.reshape(rows, head_count * HD)
    attended = row_order(attended)
    return jnp.dot(attended, w_out, preferred_element_type=jnp.float32)


def on_device(
    latent,
    control_latent,
    patch_tiles,
    tile_lists,
    tile_counts,
    embed_weight,
    control_embed,
    modulation,
    qk_gain,
    qkv_weight,
    out_weight,
    stale_cache,
    control_gain,
    final_mod,
    final_weight,
):
    section_size = lax.axis_size("section")
    slot_count = section_size // HG
    pair_count = slot_count // 2
    pair_size = 2 * HG
    device_index = lax.axis_index("section")
    slot_index = device_index // HG
    group_index = device_index % HG
    parity = slot_index % 2
    pair_index = slot_index // 2
    position = device_index % pair_size
    group_bits = HG.bit_length() - 1
    pair_bits = pair_size.bit_length() - 1

    both = jnp.concatenate([latent, control_latent], axis=1)
    whole = lax.all_gather(both, "section", axis=0, tiled=True)
    rows = whole.shape[0]
    c_out = latent.shape[1]
    tiles = rows // TILE
    final_rows = rows // pair_size
    whole_latent = whole[:, :c_out]
    whole_condition = whole[:, c_out:]
    embedded = jnp.dot(whole_latent, embed_weight, preferred_element_type=jnp.float32)
    hidden_in = embedded.astype(jnp.bfloat16)
    control_in = (
        embedded + jnp.dot(whole_condition, control_embed, preferred_element_type=jnp.float32)
    ).astype(jnp.bfloat16)

    starts = jnp.cumsum(patch_tiles) - patch_tiles
    tile_ids = jnp.arange(tiles, dtype=jnp.int32)
    tile_patch = jnp.sum((starts[None, :] <= tile_ids[:, None]).astype(jnp.int32), axis=1) - 1

    w_qkv = qkv_weight[0]
    w_out = out_weight[0]
    stale = stale_cache[0]
    shifts = modulation[slot_index]
    gain_pair = qk_gain[slot_index]
    tile_list = tile_lists[slot_index]
    tile_limit = tile_counts[slot_index]
    gate_control = modulation[2 * pair_index, 2]
    gate_main = modulation[2 * pair_index + 1, 2]
    control_row = control_gain[pair_index]

    bit_order = list(range(group_bits))
    inverse = [0] * HG
    for group in range(HG):
        inverse[block_position(group, bit_order)] = group
    halves = pair_size // HG

    def row_order(values):
        split = values.reshape(halves, HG, final_rows, values.shape[1])
        split = split[:, jnp.array(inverse)]
        return jnp.swapaxes(split, 0, 1).reshape(values.shape)

    for stage in range(pair_count):
        stream = jnp.where(parity == 0, control_in, hidden_in)
        modded = modulated(stream, shifts[0], shifts[1])
        partial = attend_all(
            modded, w_qkv, w_out, stale, gain_pair, tile_patch, tile_list, tile_limit, row_order
        ).astype(jnp.bfloat16)
        summed = reduce_rows(partial, group_index, bit_order)
        kept = lax.dynamic_slice_in_dim(summed, parity * final_rows, final_rows, 0)
        given = lax.dynamic_slice_in_dim(summed, (1 - parity) * final_rows, final_rows, 0)
        received = from_partner(given.astype(jnp.bfloat16), "section", group_bits).astype(
            jnp.float32
        )
        sum_control = jnp.where(parity == 0, kept, received)
        sum_main = jnp.where(parity == 0, received, kept)
        own_start = position * final_rows
        control_rows = lax.dynamic_slice_in_dim(control_in, own_start, final_rows, 0)
        hidden_rows = lax.dynamic_slice_in_dim(hidden_in, own_start, final_rows, 0)
        control_new = (control_rows.astype(jnp.float32) + gate_control * sum_control).astype(
            jnp.bfloat16
        )
        hidden_new = (
            hidden_rows.astype(jnp.float32)
            + gate_main * sum_main
            + control_row * control_new.astype(jnp.float32)
        ).astype(jnp.bfloat16)
        if stage + 1 < pair_count:
            moved = from_behind((control_new, hidden_new), "section", pair_size)
            control_in = gather_rows(moved[0], position, pair_bits)
            hidden_in = gather_rows(moved[1], position, pair_bits)

    denoised = jnp.dot(
        modulated(hidden_new, final_mod[0], final_mod[1]),
        final_weight,
        preferred_element_type=jnp.float32,
    )
    if pair_count == 1:
        return denoised
    is_last = pair_index == pair_count - 1
    placed = lax.dynamic_update_slice_in_dim(
        jnp.zeros((rows, denoised.shape[1]), jnp.float32),
        jnp.where(is_last, denoised, 0.0),
        position * final_rows,
        0,
    )
    return lax.psum_scatter(placed, "section", scatter_dimension=0, tiled=True)


def solution(mesh):
    return jax.shard_map(
        on_device,
        mesh=mesh,
        in_specs=(
            P(("grp", "section"), None),
            P(("grp", "section"), None),
            P(),
            P(),
            P(),
            P(),
            P(),
            P(),
            P(),
            P("section", None, None),
            P("section", None, None),
            P("section", "grp", None),
            P(),
            P(),
            P(),
        ),
        out_specs=P(("grp", "section"), None),
        check_vma=False,
    )
```

time: 694 us -> 217 us (0.31)
  waiting for transfers between devices: 351 us -> 61.2 us
  starting transfers between devices: 121 us -> 0.48 us
  matrix products: 75.3 us -> 26.8 us
  local copies, waits for them, and re-layouts: 38.4 us -> 72 us
  blocking collectives: 41.6 us -> 23.6 us
  between operations: 13.5 us -> 0.29 us
  loops' own time: 13 us -> 0 us
    ppermute x30 -> x4, waiting for transfers between devices: 261 us -> 61.2 us  [from_partner(): lax.ppermute(value, axis, [(i, i ^ 1 << distance) for i in range(lax.axis...]
    reduce_scatter x1 -> x0, waiting for transfers between devices: 66.3 us -> none  [on_device(): lax.psum_scatter(finished[3][:seq_rows], 'section', scatter_dimension=0,...]
    ppermute x30 -> x4, starting transfers between devices: 64 us -> 0.48 us  [from_partner(): lax.ppermute(value, axis, [(i, i ^ 1 << distance) for i in range(lax.axis...]
    ppermute x10 -> x0, starting transfers between devices: 57.5 us -> none  [from_behind(): lax.ppermute(value, axis, [(source, source + steps) for source in range(l...]
    dot_general x31 -> x7, matrix products: 72.4 us -> 26.8 us  [the longest x1 9.83 us: attend_all(): jnp.dot(modded, w_qkv, preferred_element_type=jnp.float32)]
    ppermute x10 -> x0, waiting for transfers between devices: 23.7 us -> none  [from_behind(): lax.ppermute(value, axis, [(source, source + steps) for source in range(l...]
    all_gather x2 -> x1, blocking collectives: 41.6 us -> 23.6 us  [on_device(): whole = lax.all_gather(both, 'section', axis=0, tiled=True)]
    unnamed x20 -> x27, local copies, waits for them, and re-layouts: 1.65 us -> 16 us
  transfers between devices with their start and end apart: 41 -> 4, of which waited for: 41 -> 4; matrix products, arithmetic and copies ran while one was open for 2% -> 1% of each run, Pallas kernels for 0% -> 0%
where the time goes in v1:
time: 217 us; the launch traced here: 215 us
  local copies, waits for them, and re-layouts  72 us (33%)
  waiting for transfers between devices  61.2 us (28%)
  other arithmetic  30.8 us (14%)
  matrix products  26.8 us (12%)
  blocking collectives  23.6 us (11%)
    ppermute x4, waiting for transfers between devices, from_partner(): lax.ppermute(value, axis, [(i, i ^ 1 << distance) for i in range(lax.axis...  61.2 us
    all_gather x1, blocking collectives, on_device(): whole = lax.all_gather(both, 'section', axis=0, tiled=True)  23.6 us
    unnamed x27, local copies, waits for them, and re-layouts  16 us
    dot_general x1, matrix products, attend_all(): jnp.dot(modded, w_qkv, preferred_element_type=jnp.float32)  9.83 us
    mul x5, local copies, waits for them, and re-layouts, rms_scaled(): values * lax.rsqrt(jnp.mean(values * values, axis=-1, keepdims=True) + EP...  7.56 us
    add x3, other arithmetic, reduce_rows(): current = kept.astype(jnp.float32) + received.astype(jnp.float32)  7.05 us
    reshape x1, local copies, waits for them, and re-layouts, attend_all(): chosen[..., :head_count * HD].reshape(tiles, ksel * TILE, head_count, HD)  5.84 us
    reshape x1, local copies, waits for them, and re-layouts, attend_all(): chosen[..., head_count * HD:].reshape(tiles, ksel * TILE, head_count, HD)  5.56 us
  transfers between devices with their start and end apart: 4, of which 4 were waited for; matrix products, arithmetic and copies ran while one was open for 1% of the time, Pallas kernels for 0%

profile of v1, /device:TPU:0, one launch (start us, length us, event | category | flops | bytes accessed | tf_op | source)
XLA Modules:
  0.0 215.2 jit_solution(11525362747779159308)
XLA Ops:
  1.0 23.6 %all_gather.3 = bf16[768,128]{1,0:T(8,128)(2,1)S(1)} all-gather(bf16[48,128]{1,0:T(8,128)(2,1)S(1)} %pad_maximum_fusion.1), channel_id=1, replica_groups=mesh['grp'=2,'section'=16] {'section'}, dimensions={0}, use_global_device_ids=true | all-gather | bytes 208896 | tf_op jit(solution)/shard_map/all_gather | solution.py:147
  24.6 10.3 %copy.49 = bf16[1,3072,1152]{1,2,0:T(8,128)(2,1)} copy(bf16[1,3072,1152]{2,1,0:T(8,128)(2,1)} %param.25) | data formatting | bytes 14155776 | tf_op args[9]
  34.9 1.4 fusion.54
  36.3 4.7 %convert_reduce_fusion = (f32[768]{0:T(1024)S(1)}, bf16[768,3072]{1,0:T(8,128)(2,1)S(1)}, bf16[768,3072]{1,0:T(8,128)(2,1)}, bf16[768,3072]{1,0:T(8,128)(2,1)}) fusion(pred[]{:T(512)S(6)} %eq.9, f32[768,3072]{1,0:T(8,128)S(1)} %fusion.54, bf16[64,3072]{1,0:T(8,128)(2,1)S(1)} %copy-done.8, bf16[768,128]{1,0:T(8,128)(2,1)S(1)} %all_gather.3), kind=kOutput, calls=%fused_computation.5 | convolution fusion | flops 316144896 | bytes 24185856 | tf_op jit(solution)/shard_map/dot_general | solution.py:157
  41.0 2.1 copy-done.1
  43.1 1.4 fusion.3
  45.1 9.8 %fusion.8 = f32[768,3,3,128]{3,0,2,1:T(8,128)S(1)} fusion(bf16[3,3,128,3072]{3,2,1,0:T(8,128)(2,1)} %bitcast.65, bf16[768,3072]{1,0:T(8,128)(2,1)} %copy-done.1, f32[3072]{0:T(1024)S(1)} %bitcast.73, f32[3072]{0:T(1024)S(1)} %bitcast.72, f32[768]{0:T(1024)S(1)} %add_rsqrt_fusion.1, f32[768]{0:T(1024)S(1)} %broadcast_multiply_fusion), kind=kOutput, calls=%fused_computation.15 | convolution fusion | flops 5449973760 | bytes 15366144 | tf_op jit(solution)/shard_map/dot_general | solution.py:80
  55.9 2.1 multiply_reduce_fusion
  58.6 2.5 %copy.65 = bf16[768,1,3,128]{3,2,0,1:T(4,128)(2,1)} copy(bf16[768,1,3,128]{3,0,2,1:T(8,128)(2,1)} %slice.80) | data formatting | bytes 1179648 | tf_op jit(solution)/shard_map/convert_element_type | solution.py:85
  61.1 2.6 %reshape.281 = bf16[6,128,384]{2,1,0:T(8,128)(2,1)} reshape(bf16[768,1,3,128]{3,2,0,1:T(4,128)(2,1)} %copy.65) | data formatting | bytes 1179648 | tf_op jit(solution)/shard_map/convert_element_type | solution.py:85
  63.7 2.0 copy.64
  65.7 2.2 %reshape.280 = f32[6,128,384]{2,1,0:T(8,128)S(1)} reshape(f32[768,1,3,128]{3,2,0,1:T(4,128)} %copy.64) | data formatting | bytes 2359296 | tf_op jit(solution)/shard_map/squeeze | solution.py:84
  69.8 2.5 %mul.168 = f32[6,128,384]{1,0,2:T(8,128)} reshape(f32[768,3,128]{0,2,1:T(8,128)} %mul.167) | data formatting | bytes 2359296 | tf_op jit(solution)/shard_map/mul | solution.py:35
  72.3 2.8 %copy.52 = f32[6,128,384]{2,1,0:T(8,128)} copy(f32[6,128,384]{1,0,2:T(8,128)} %mul.168) | data formatting | bytes 2359296 | tf_op jit(solution)/shard_map/mul | solution.py:35
  77.8 1.3 compare_select_fusion.1
  79.1 1.3 copy.55
  80.4 1.3 reshape.254
  83.0 1.4 gather_fusion
  84.3 1.3 gather.12
  85.6 1.3 copy.56
  86.9 1.3 compare_select_fusion
  90.4 1.5 multiply_convert_fusion
  91.9 2.7 %pad_maximum_fusion = bf16[12,128,768]{2,1,0:T(8,128)(2,1)} fusion(bf16[6,128,768]{2,1,0:T(8,128)(2,1)S(1)} %bitcast.67, bf16[6,128,384]{2,1,0:T(8,128)(2,1)} %reshape.281, bf16[6,128,384]{2,1,0:T(8,128)(2,1)S(1)} %multiply_convert_fusion), kind=kLoop, calls=%fused_computation.26 | loop fusion | flops 7077888 | bytes 4718592 | tf_op jit(solution)/shard_map/concatenate | solution.py:91
  94.6 4.5 %gather_fusion.1 = bf16[18,128,768]{2,1,0:T(8,128)(2,1)} fusion(bf16[12,128,768]{2,1,0:T(8,128)(2,1)} %pad_maximum_fusion, s32[1024]{0:T(1024)S(1)} %pad_clamp_fusion.1), kind=kCustom, calls=%fused_computation.1 | custom fusion | bytes 7077960 | tf_op jit(solution)/shard_map/gather | solution.py:96
  99.0 4.4 %fusion.65 = (bf16[6,3,128,384]{3,2,1,0:T(8,128)(2,1)}, bf16[6,3,128,384]{3,2,1,0:T(8,128)(2,1)}) fusion(bf16[6,3,128,768]{3,2,1,0:T(8,128)(2,1)} %bitcast.64), kind=kLoop, calls=%fused_computation.118 | loop fusion | bytes 7077888 | tf_op jit(solution)/shard_map/slice | solution.py:98
  103.4 5.8 %reshape.250 = bf16[6,384,3,128]{3,2,1,0:T(4,128)(2,1)} reshape(bf16[6,3,128,384]{3,2,1,0:T(8,128)(2,1)} %get-tuple-element.13) | data formatting | bytes 3538944 | tf_op jit(solution)/shard_map/reshape | solution.py:97
  109.3 1.3 rsqrt_bitcast_fusion
  110.6 1.3 fusion.61
  111.8 5.6 %reshape.249 = bf16[6,384,3,128]{3,2,1,0:T(4,128)(2,1)} reshape(bf16[6,3,128,384]{3,2,1,0:T(8,128)(2,1)} %get-tuple-element.12) | data formatting | bytes 3538944 | tf_op jit(solution)/shard_map/reshape | solution.py:98
  118.1 2.6 %fusion.18 = f32[6,3,128,384]{3,2,1,0:T(8,128)S(1)} fusion(bf16[6,384,3,128]{3,2,1,0:T(4,128)(2,1)} %reshape.250, f32[6,128,3,128]{3,1,0,2:T(8,128)S(1)} %bitcast.66, f32[128]{0:T(128)} %get-tuple-element.22, f32[6,128,3]{1,2,0:T(4,128)} %rsqrt_bitcast_fusion), kind=kOutput, calls=%fused_computation.32 | convolution fusion | flops 227377152 | bytes 6497792 | tf_op jit(solution)/shard_map/tqhd,tkhd->thqk/dot_general | solution.py:100
  120.7 1.8 fusion.66
  122.5 2.0 fusion.26
  124.6 1.5 copy.62
  127.3 1.7 gather_fusion.2
  129.1 4.3 %convolution_convert_fusion = bf16[768,3072]{1,0:T(8,128)(2,1)} fusion(bf16[768,384]{1,0:T(8,128)(2,1)S(1)} %bitcast.68, bf16[1,384,3072]{2,1,0:T(8,128)(2,1)S(1)} %copy-done), kind=kOutput, calls=%fused_computation.13 | convolution fusion | flops 1814298624 | bytes 7667712 | tf_op jit(solution)/shard_map/dot_general | solution.py:113
  133.3 3.2 %constant_dynamic-slice_fusion = bf16[384,3072]{1,0:T(8,128)(2,1)} fusion(bf16[768,3072]{1,0:T(8,128)(2,1)} %convolution_convert_fusion, s32[]{:T(128)S(6)} %select_n.148), kind=kLoop, calls=%fused_computation.85 | loop fusion | bytes 4718596 | tf_op jit(solution)/shard_map/dynamic_slice | solution.py:54
  136.9 4.5 %collective-permute-done = bf16[384,3072]{1,0:T(8,128)(2,1)} collective-permute-done((bf16[384,3072]{1,0:T(8,128)(2,1)}, bf16[384,3072]{1,0:T(8,128)(2,1)}, u32[]{:S(2)}, u32[]{:S(2)}) %collective-permute-start) | collective-permute-done | bytes 2359328 | tf_op jit(solution)/shard_map/ppermute | solution.py:16
  141.5 3.2 %convert_add_fusion = f32[384,3072]{1,0:T(8,128)S(1)} fusion(bf16[384,3072]{1,0:T(8,128)(2,1)} %collective-permute-done, bf16[768,3072]{1,0:T(8,128)(2,1)} %convolution_convert_fusion, s32[]{:T(128)S(6)} %select_n.147), kind=kLoop, calls=%fused_computation.16 | loop fusion | flops 3538944 | bytes 9437188 | tf_op jit(solution)/shard_map/add | solution.py:58
  144.7 2.1 copy-done.2
  147.1 28.3 %collective-permute-done.1 = bf16[192,3072]{1,0:T(8,128)(2,1)} collective-permute-done((bf16[192,3072]{1,0:T(8,128)(2,1)S(1)}, bf16[192,3072]{1,0:T(8,128)(2,1)}, u32[]{:S(2)}, u32[]{:S(2)}) %collective-permute-start.1) | collective-permute-done | bytes 1179680 | tf_op jit(solution)/shard_map/ppermute | solution.py:16
  175.3 2.3 %convert_add_fusion.1 = f32[192,3072]{1,0:T(8,128)S(1)} fusion(bf16[192,3072]{1,0:T(8,128)(2,1)} %collective-permute-done.1, f32[384,3072]{1,0:T(8,128)} %copy-done.2, s32[]{:T(128)S(6)} %select_n.149), kind=kLoop, calls=%fused_computation.28 | loop fusion | flops 1179648 | bytes 5898244 | tf_op jit(solution)/shard_map/add | solution.py:58
  177.6 1.4 copy-done.3
  179.2 14.8 %collective-permute-done.2 = bf16[96,3072]{1,0:T(8,128)(2,1)} collective-permute-done((bf16[96,3072]{1,0:T(8,128)(2,1)S(1)}, bf16[96,3072]{1,0:T(8,128)(2,1)}, u32[]{:S(2)}, u32[]{:S(2)}) %collective-permute-start.2) | collective-permute-done | bytes 589856 | tf_op jit(solution)/shard_map/ppermute | solution.py:16
  194.0 1.6 convert_add_fusion.2
  196.3 1.4 slice_add_fusion
  197.8 13.6 %collective-permute-done.3 = bf16[48,3072]{1,0:T(8,128)(2,1)} collective-permute-done((bf16[48,3072]{1,0:T(8,128)(2,1)}, bf16[48,3072]{1,0:T(8,128)(2,1)}, u32[]{:S(2)}, u32[]{:S(2)}) %collective-permute-start.3) | collective-permute-done | bytes 294944 | tf_op jit(solution)/shard_map/ppermute | solution.py:16
  211.4 1.5 convert_reduce_fusion.1
  213.2 2.0 fusion.47
  (55 shorter events, 14.8 us)
Async XLA Ops:
  0.0 129.1 %copy-start = (bf16[1,384,3072]{2,1,0:T(8,128)(2,1)S(1)}, bf16[1,384,3072]{2,1,0:T(8,128)(2,1)}, u32[]{:S(2)}) copy-start(bf16[1,384,3072]{2,1,0:T(8,128)(2,1)} %param.26) | copy-start | bytes 7077892
  24.6 10.3 %copy-start.7 = (bf16[64,3072]{1,0:T(8,128)(2,1)S(1)}, bf16[64,3072]{1,0:T(8,128)(2,1)}, u32[]{:S(2)}) copy-start(bf16[64,3072]{1,0:T(8,128)(2,1)} %param.21) | copy-start | bytes 1179652
  34.9 1.4 copy-start.8
  41.0 2.1 copy-start.1
  41.0 3.5 %copy-start.9 = (f32[2,3,3072]{2,0,1:T(2,128)S(1)}, f32[2,3,3072]{2,0,1:T(2,128)}, u32[]{:S(2)}) copy-start(f32[2,3,3072]{2,0,1:T(2,128)} %param.23) | copy-start | bytes 221188
  67.9 7.1 %copy-start.12 = (f32[2,2,128]{2,1,0:T(2,128)S(1)}, f32[2,2,128]{2,1,0:T(2,128)}, u32[]{:S(2)}) copy-start(f32[2,2,128]{2,1,0:T(2,128)} %param.24) | copy-start | bytes 6148
  89.6 2.2 %copy-start.6 = (bf16[1,768,768]{2,1,0:T(8,128)(2,1)S(1)}, bf16[1,768,768]{2,1,0:T(8,128)(2,1)}, u32[]{:S(2)}) copy-start(bf16[1,768,768]{2,1,0:T(8,128)(2,1)} %param.27) | copy-start | bytes 3538948
  103.4 14.0 %copy-start.10 = (s32[384]{0:T(512)S(1)}, s32[384]{0:T(512)}, u32[]{:S(2)}) copy-start(s32[384]{0:T(512)} %add_select_fusion) | copy-start | bytes 4612
  103.4 14.7 %copy-start.4 = (f32[768,1,3,128]{3,0,2,1:T(8,128)S(1)}, f32[768,1,3,128]{3,0,2,1:T(8,128)}, u32[]{:S(2)}) copy-start(f32[768,1,3,128]{3,0,2,1:T(8,128)} %get-tuple-element.14) | copy-start | bytes 3538948
  120.7 1.8 copy-start.5
  122.5 4.8 %copy-start.11 = (s32[8]{0:T(128)S(1)}, s32[8]{0:T(128)}, u32[]{:S(2)}) copy-start(s32[8]{0:T(128)} %constant.135) | copy-start | bytes 100
  136.6 4.9 %collective-permute-start = (bf16[384,3072]{1,0:T(8,128)(2,1)}, bf16[384,3072]{1,0:T(8,128)(2,1)}, u32[]{:S(2)}, u32[]{:S(2)}) collective-permute-start(bf16[384,3072]{1,0:T(8,128)(2,1)} %constant_dynamic-slice_fusion), channel_id=1, source_target_pairs={{0,1},{1,0},{2,3},{3,2},{4,5},{5,4},{6,7},{7,6},{8,9},{9,8},{10,11... | collective-permute-start | bytes 7077896 | tf_op jit(solution)/shard_map/ppermute | solution.py:16
  144.7 2.1 copy-start.2
  147.0 28.4 %collective-permute-start.1 = (bf16[192,3072]{1,0:T(8,128)(2,1)S(1)}, bf16[192,3072]{1,0:T(8,128)(2,1)}, u32[]{:S(2)}, u32[]{:S(2)}) collective-permute-start(bf16[192,3072]{1,0:T(8,128)(2,1)S(1)} %dynamic-slice_convert_fusion), channel_id=1, source_target_pairs={{0,2},{1,3},{2,0},{3,1},{4,6},{5,7},{6,4},{7,5},{8,10},{9,11},{10,... | collective-permute-start | bytes 3538952 | tf_op jit(solution)/shard_map/ppermute | solution.py:16
  177.6 1.4 copy-start.3
  179.1 14.9 %collective-permute-start.2 = (bf16[96,3072]{1,0:T(8,128)(2,1)S(1)}, bf16[96,3072]{1,0:T(8,128)(2,1)}, u32[]{:S(2)}, u32[]{:S(2)}) collective-permute-start(bf16[96,3072]{1,0:T(8,128)(2,1)S(1)} %dynamic-slice_convert_fusion.1), channel_id=1, source_target_pairs={{0,4},{1,5},{2,6},{3,7},{4,0},{5,1},{6,2},{7,3},{8,12},{9,13},{10,... | collective-permute-start | bytes 1769480 | tf_op jit(solution)/shard_map/ppermute | solution.py:16
  196.3 15.1 %collective-permute-start.3 = (bf16[48,3072]{1,0:T(8,128)(2,1)}, bf16[48,3072]{1,0:T(8,128)(2,1)}, u32[]{:S(2)}, u32[]{:S(2)}) collective-permute-start(bf16[48,3072]{1,0:T(8,128)(2,1)} %dynamic-slice_convert_fusion.2), channel_id=1, source_target_pairs={{0,8},{1,9},{2,10},{3,11},{4,12},{5,13},{6,14},{7,15},{8,0},{9,1},... | collective-permute-start | bytes 884744 | tf_op jit(solution)/shard_map/ppermute | solution.py:16

commit v2 on v1

v2 whole, which is shorter than its diff:
```python
import math

import jax
import jax.numpy as jnp
from jax import lax
from jax.experimental import pallas as pl
from jax.experimental.pallas import tpu as pltpu
from jax.sharding import PartitionSpec as P

HD = 128
HG = 8
TILE = 128

EPSILON = 1e-06


def from_partner(value, axis, distance):
    return lax.ppermute(value, axis, [(i, i ^ 1 << distance) for i in range(lax.axis_size(axis))])


def from_behind(value, axis, steps):
    count = lax.axis_size(axis)
    leading, last = (max(0, -steps), min(count, count - steps))
    return lax.ppermute(value, axis, [(source, source + steps) for source in range(leading, last)])


def modulated(hidden, shift_row, scale_row):
    values = hidden.astype(jnp.float32)
    centered = values - jnp.mean(values, axis=-1, keepdims=True)
    variance = jnp.mean(centered * centered, axis=-1, keepdims=True)
    normed = centered * lax.rsqrt(variance + EPSILON)
    return (normed * (1.0 + scale_row) + shift_row).astype(jnp.bfloat16)


def rms_scaled(values, gain_row):
    return (
        values * lax.rsqrt(jnp.mean(values * values, axis=-1, keepdims=True) + EPSILON) * gain_row
    )


def bit_of(value, bit):
    return (value >> bit) & 1


def gather_rows(mine, position, bit_count):
    gathered = mine
    for bit in range(bit_count):
        partner = from_partner(gathered, "section", bit)
        upper = bit_of(position, bit) == 1
        gathered = jnp.where(
            upper,
            jnp.concatenate([partner, gathered]),
            jnp.concatenate([gathered, partner]),
        )
    return gathered


def qkv_kernel(x_ref, w_ref, g_ref, o_ref):
    j = pl.program_id(0)
    acc = jnp.dot(x_ref[...], w_ref[...], preferred_element_type=jnp.float32)
    gain = g_ref[pl.ds(jnp.minimum(j, 1), 1), :]
    heads = acc.shape[1] // HD
    pieces = []
    for h in range(heads):
        values = acc[:, h * HD : (h + 1) * HD]
        scaled = values * lax.rsqrt(jnp.mean(values * values, axis=-1, keepdims=True) + EPSILON) * gain
        pieces.append(jnp.where(j < 2, scaled, values))
    o_ref[...] = jnp.concatenate(pieces, axis=1).astype(o_ref.dtype)


def project_qkv(modded, w_qkv, gain_pair):
    rows, depth = modded.shape
    width = w_qkv.shape[1] // 3
    return pl.pallas_call(
        qkv_kernel,
        out_shape=jax.ShapeDtypeStruct((rows, 3 * width), jnp.bfloat16),
        grid=(3,),
        in_specs=[
            pl.BlockSpec((rows, depth), lambda j: (0, 0)),
            pl.BlockSpec((depth, width), lambda j: (0, j)),
            pl.BlockSpec((2, HD), lambda j: (0, 0)),
        ],
        out_specs=pl.BlockSpec((rows, width), lambda j: (0, j)),
        compiler_params=pltpu.CompilerParams(vmem_limit_bytes=48 * 1024 * 1024),
        cost_estimate=pl.CostEstimate(
            flops=2 * rows * depth * 3 * width,
            bytes_accessed=2 * (rows * depth + depth * 3 * width + rows * 3 * width),
            transcendentals=0,
        ),
    )(modded, w_qkv, gain_pair)


def attention_kernel(picked_ref, limit_ref, q_ref, m0_ref, m1_ref, m2_ref, o_ref):
    t = pl.program_id(0)
    limit = limit_ref[t]
    width = q_ref.shape[1]
    heads = width // HD
    memories = (m0_ref, m1_ref, m2_ref)
    for h in range(heads):
        query = q_ref[:, h * HD : (h + 1) * HD]
        scores = []
        for j, m_ref in enumerate(memories):
            key = m_ref[:, h * HD : (h + 1) * HD]
            s = lax.dot_general(
                query, key, (((1,), (1,)), ((), ())), preferred_element_type=jnp.float32
            ) / math.sqrt(HD)
            scores.append(jnp.where(j < limit, s, -1e30))
        highest = jnp.max(scores[0], axis=-1, keepdims=True)
        for s in scores[1:]:
            highest = jnp.maximum(highest, jnp.max(s, axis=-1, keepdims=True))
        weights = [jnp.exp(s - highest) for s in scores]
        total = jnp.sum(weights[0], axis=-1, keepdims=True)
        for w in weights[1:]:
            total = total + jnp.sum(w, axis=-1, keepdims=True)
        acc = None
        for w, m_ref in zip(weights, memories):
            probabilities = (w / total).astype(jnp.bfloat16)
            value = m_ref[:, width + h * HD : width + (h + 1) * HD]
            part = jnp.dot(probabilities, value, preferred_element_type=jnp.float32)
            acc = part if acc is None else acc + part
        o_ref[:, h * HD : (h + 1) * HD] = acc.astype(o_ref.dtype)


def attend_tiles(projected, memory, picked, limit):
    rows = projected.shape[0]
    width = projected.shape[1] // 3
    tiles = rows // TILE
    mem_width = memory.shape[1]

    def memory_spec(j):
        return pl.BlockSpec((TILE, mem_width), lambda t, p, c: (p[t, j], 0))

    return pl.pallas_call(
        attention_kernel,
        out_shape=jax.ShapeDtypeStruct((rows, width), jnp.bfloat16),
        grid_spec=pltpu.PrefetchScalarGridSpec(
            num_scalar_prefetch=2,
            grid=(tiles,),
            in_specs=[
                pl.BlockSpec((TILE, width), lambda t, p, c: (t, 0)),
                memory_spec(0),
                memory_spec(1),
                memory_spec(2),
            ],
            out_specs=pl.BlockSpec((TILE, width), lambda t, p, c: (t, 0)),
        ),
        cost_estimate=pl.CostEstimate(
            flops=4 * rows * 3 * TILE * width,
            bytes_accessed=2 * (2 * rows * width + 3 * rows * mem_width),
            transcendentals=rows * 3 * TILE * (width // HD),
        ),
    )(picked, limit, projected, memory, memory, memory)


def row_table(group_count):
    table = []
    for g in range(group_count):
        first = [g, g ^ 4, g ^ 2, g ^ 6]
        second = [group_count + k for k in (g, g ^ 2, g ^ 4, g ^ 6)]
        own = first + second
        other = [g ^ 1, g ^ 5, g ^ 3, g ^ 7]
        other_second = [group_count + k for k in (g ^ 1, g ^ 3, g ^ 5, g ^ 7)]
        table.append(own + other + other_second)
    return table


def reduce_two_ways(partial):
    half = partial.shape[0] // 2
    summed = partial[:half].astype(jnp.float32) + from_partner(
        partial[half:], "section", 0
    ).astype(jnp.float32)
    quarter = half // 2
    first, second = summed[:quarter], summed[quarter:]
    eighth = quarter // 2
    first_sent = first[eighth:].astype(jnp.bfloat16)
    second_sent = second[eighth:].astype(jnp.bfloat16)
    first = first[:eighth] + from_partner(first_sent, "section", 1).astype(jnp.float32)
    second = second[:eighth] + from_partner(second_sent, "section", 2).astype(jnp.float32)
    sixteenth = eighth // 2
    first = first[:sixteenth] + from_partner(
        first[sixteenth:].astype(jnp.bfloat16), "section", 2
    ).astype(jnp.float32)
    second = second[:sixteenth] + from_partner(
        second[sixteenth:].astype(jnp.bfloat16), "section", 1
    ).astype(jnp.float32)
    return first, second


def on_device(
    latent,
    control_latent,
    patch_tiles,
    tile_lists,
    tile_counts,
    embed_weight,
    control_embed,
    modulation,
    qk_gain,
    qkv_weight,
    out_weight,
    stale_cache,
    control_gain,
    final_mod,
    final_weight,
):
    section_size = lax.axis_size("section")
    slot_count = section_size // HG
    pair_count = slot_count // 2
    pair_size = 2 * HG
    device_index = lax.axis_index("section")
    slot_index = device_index // HG
    group_index = device_index % HG
    parity = slot_index % 2
    pair_index = slot_index // 2
    position = device_index % pair_size
    group_bits = HG.bit_length() - 1
    pair_bits = pair_size.bit_length() - 1
    section_bits = section_size.bit_length() - 1

    both = jnp.concatenate([latent, control_latent], axis=1)
    whole = gather_rows(both, device_index, section_bits)
    rows = whole.shape[0]
    c_out = latent.shape[1]
    tiles = rows // TILE
    final_rows = rows // pair_size
    whole_latent = whole[:, :c_out]
    whole_condition = jnp.where(parity == 0, whole[:, c_out:], jnp.zeros_like(whole[:, c_out:]))
    embedded = jnp.dot(whole_latent, embed_weight, preferred_element_type=jnp.float32)
    stream = (
        embedded + jnp.dot(whole_condition, control_embed, preferred_element_type=jnp.float32)
    ).astype(jnp.bfloat16)
    hidden_in = embedded.astype(jnp.bfloat16)

    starts = jnp.cumsum(patch_tiles) - patch_tiles
    tile_ids = jnp.arange(tiles, dtype=jnp.int32)
    tile_patch = jnp.sum((starts[None, :] <= tile_ids[:, None]).astype(jnp.int32), axis=1) - 1

    w_qkv = qkv_weight[0]
    w_out = out_weight[0]
    stale = stale_cache[0]
    shifts = modulation[slot_index]
    gain_pair = qk_gain[slot_index]
    tile_list = tile_lists[slot_index]
    tile_limit = tile_counts[slot_index]
    use_new = tile_patch[tile_list] <= tile_patch[:, None]
    picked = (tile_list + jnp.where(use_new, 0, tiles)).astype(jnp.int32)
    gate_control = modulation[2 * pair_index, 2]
    gate_main = modulation[2 * pair_index + 1, 2]
    control_row = control_gain[pair_index]
    order = jnp.array(row_table(HG), jnp.int32)[group_index]

    for stage in range(pair_count):
        modded = modulated(stream, shifts[0], shifts[1])
        projected = project_qkv(modded, w_qkv, gain_pair)
        width = projected.shape[1] // 3
        memory = jnp.concatenate([projected[:, width:], stale], axis=0)
        attended = attend_tiles(projected, memory, picked, tile_limit.astype(jnp.int32))
        attended = attended.reshape(pair_size, final_rows, width)[order].reshape(rows, width)
        partial = jnp.dot(attended, w_out, preferred_element_type=jnp.float32).astype(
            jnp.bfloat16
        )
        first, second = reduce_two_ways(partial)
        kept = jnp.where(parity == 0, first, second)
        given = jnp.where(parity == 0, second, first)
        received = from_partner(given.astype(jnp.bfloat16), "section", group_bits).astype(
            jnp.float32
        )
        sum_control = jnp.where(parity == 0, kept, received)
        sum_main = jnp.where(parity == 0, received, kept)
        own_start = position * final_rows
        if stage == 0:
            latent_rows = lax.dynamic_slice_in_dim(whole, own_start, final_rows, 0)
            own_embedded = jnp.dot(
                latent_rows[:, :c_out], embed_weight, preferred_element_type=jnp.float32
            )
            control_rows = (
                own_embedded
                + jnp.dot(latent_rows[:, c_out:], control_embed, preferred_element_type=jnp.float32)
            ).astype(jnp.bfloat16)
            hidden_rows = own_embedded.astype(jnp.bfloat16)
        else:
            control_rows = lax.dynamic_slice_in_dim(control_in, own_start, final_rows, 0)
            hidden_rows = lax.dynamic_slice_in_dim(hidden_in, own_start, final_rows, 0)
        control_new = (control_rows.astype(jnp.float32) + gate_control * sum_control).astype(
            jnp.bfloat16
        )
        hidden_new = (
            hidden_rows.astype(jnp.float32)
            + gate_main * sum_main
            + control_row * control_new.astype(jnp.float32)
        ).astype(jnp.bfloat16)
        if stage + 1 < pair_count:
            moved = from_behind((control_new, hidden_new), "section", pair_size)
            control_in = gather_rows(moved[0], position, pair_bits)
            hidden_in = gather_rows(moved[1], position, pair_bits)
            stream = jnp.where(parity == 0, control_in, hidden_in)

    denoised = jnp.dot(
        modulated(hidden_new, final_mod[0], final_mod[1]),
        final_weight,
        preferred_element_type=jnp.float32,
    )
    if pair_count == 1:
        return denoised
    is_last = pair_index == pair_count - 1
    placed = lax.dynamic_update_slice_in_dim(
        jnp.zeros((rows, denoised.shape[1]), jnp.float32),
        jnp.where(is_last, denoised, 0.0),
        position * final_rows,
        0,
    )
    return lax.psum_scatter(placed, "section", scatter_dimension=0, tiled=True)


def solution(mesh):
    return jax.shard_map(
        on_device,
        mesh=mesh,
        in_specs=(
            P(("grp", "section"), None),
            P(("grp", "section"), None),
            P(),
            P(),
            P(),
            P(),
            P(),
            P(),
            P(),
            P("section", None, None),
            P("section", None, None),
            P("section", "grp", None),
            P(),
            P(),
            P(),
        ),
        out_specs=P(("grp", "section"), None),
        check_vma=False,
    )
```

time: 217 us -> 116 us (0.53)
  local copies, waits for them, and re-layouts: 72 us -> 5.65 us
  blocking collectives: 23.6 us -> 0 us
  Pallas kernels: 0 us -> 22.7 us
  waiting for transfers between devices: 61.2 us -> 40.4 us
  starting transfers between devices: 0.48 us -> 17.5 us
  matrix products: 26.8 us -> 11 us
  other arithmetic: 30.8 us -> 17.7 us
    all_gather x1 -> x0, blocking collectives: 23.6 us -> none  [on_device(): whole = lax.all_gather(both, 'section', axis=0, tiled=True)]
    pallas_call x0 -> x2, Pallas kernels: none -> 22.7 us  [the longest x1 11.7 us: project_qkv(): pl.pallas_call(qkv_kernel, out_shape=jax.ShapeDtypeStruct((rows, 3 * widt...]
    ppermute x4 -> x10, waiting for transfers between devices: 61.2 us -> 40.4 us  [from_partner(): lax.ppermute(value, axis, [(i, i ^ 1 << distance) for i in range(lax.axis...]
    ppermute x4 -> x10, starting transfers between devices: 0.48 us -> 17.5 us  [from_partner(): lax.ppermute(value, axis, [(i, i ^ 1 << distance) for i in range(lax.axis...]
    unnamed x27 -> x22, local copies, waits for them, and re-layouts: 16 us -> 1.24 us
    dot_general x4 -> x3, matrix products: 18.7 us -> 6.1 us  [the longest x1 2.82 us: on_device(): jnp.dot(attended, w_out, preferred_element_type=jnp.float32)]
    reshape x2 -> x0, local copies, waits for them, and re-layouts: 11.4 us -> none  [the longest x1 5.84 us: attend_all(): chosen[..., :head_count * HD].reshape(tiles, ksel * TILE, head_count, HD)]
    gather x5 -> x3, local copies, waits for them, and re-layouts: 10.2 us -> 2.51 us  [the longest x1 1.73 us: on_device(): attended.reshape(pair_size, final_rows, width)[order].reshape(rows, width)]
  transfers between devices with their start and end apart: 4 -> 10, of which waited for: 4 -> 9; matrix products, arithmetic and copies ran while one was open for 1% -> 8% of each run, Pallas kernels for 0% -> 0%
where the time goes in v2:
time: 116 us; the launch traced here: 115 us
  waiting for transfers between devices  40.4 us (35%)
  Pallas kernels  22.7 us (20%)
  other arithmetic  17.7 us (15%)
  starting transfers between devices  17.5 us (15%)
  matrix products  11 us (9%)
  local copies, waits for them, and re-layouts  5.65 us (5%)
    ppermute x10, waiting for transfers between devices, from_partner(): lax.ppermute(value, axis, [(i, i ^ 1 << distance) for i in range(lax.axis...  40.4 us
    ppermute x10, starting transfers between devices, from_partner(): lax.ppermute(value, axis, [(i, i ^ 1 << distance) for i in range(lax.axis...  17.5 us
    pallas_call x1, Pallas kernels, project_qkv(): pl.pallas_call(qkv_kernel, out_shape=jax.ShapeDtypeStruct((rows, 3 * widt...  11.7 us
    pallas_call x1, Pallas kernels, attend_tiles(): pl.pallas_call(attention_kernel, out_shape=jax.ShapeDtypeStruct((rows, wi...  10.9 us
    convert_element_type x1, other arithmetic, modulated(): return (normed * (1.0 + scale_row) + shift_row).astype(jnp.bfloat16)  4.8 us
    dot_general x1, matrix products, on_device(): jnp.dot(attended, w_out, preferred_element_type=jnp.float32)  2.82 us
  transfers between devices with their start and end apart: 10, of which 9 were waited for; matrix products, arithmetic and copies ran while one was open for 8% of the time, Pallas kernels for 0%

profile of v2, /device:TPU:0, one launch (start us, length us, event | category | flops | bytes accessed | tf_op | source)
XLA Modules:
  0.0 115.1 jit_solution(13954421685144325708)
XLA Ops:
  0.0 1.0 pad_maximum_fusion.1
  1.0 0.5 collective-permute-start
  1.5 0.7 compare_select_fusion
  2.3 0.8 reduce-window.9
  3.2 0.7 bitcast_subtract_fusion
  3.9 0.7 gather_fusion
  4.8 0.7 bitcast_add_fusion.picked_ref
  5.5 1.5 %constant_dynamic-slice_fusion.6 = (f32[1,1,3072]{2,0,1:T(1,128)S(1)}, f32[1,1,3072]{2,0,1:T(1,128)S(1)}, f32[1,1,3072]{2,0,1:T(1,128)}, f32[1,1,3072]{2,0,1:T(1,128)S(1)}) fusion(f32[2,3,3072]{2,0,1:T(2,128)} %param.23, s32[]{:T(128)S(6)} %select_n.137, s32[]{:T(128)S(6)} %select_n.140, s32[]{:T(128)S(6)} %add.185, s32[]{:T(128)S(6)} %select_n.151), kind=kLoop, calls=%fused_computation.77 | loop fusion | flops 3072 | bytes 98320 | tf_op jit(solution)/shard_map/dynamic_slice | solution.py:248
  6.9 0.7 fusion.41
  7.6 0.9 maximum_select_fusion.3
  8.5 2.6 %collective-permute-start.1 = (bf16[96,128]{1,0:T(8,128)(2,1)S(1)}, bf16[96,128]{1,0:T(8,128)(2,1)S(1)}, u32[]{:S(2)}, u32[]{:S(2)}) collective-permute-start(bf16[96,128]{1,0:T(8,128)(2,1)S(1)} %maximum_select_fusion.3), channel_id=1, source_target_pairs={{0,2},{1,3},{2,0},{3,1},{4,6},{5,7},{6,4},{7,5},{8,10},{9,11},{10,... | collective-permute-start | bytes 73736 | tf_op jit(solution)/shard_map/ppermute | solution.py:18
  11.1 1.8 %collective-permute-done.1 = bf16[96,128]{1,0:T(8,128)(2,1)S(1)} collective-permute-done((bf16[96,128]{1,0:T(8,128)(2,1)S(1)}, bf16[96,128]{1,0:T(8,128)(2,1)S(1)}, u32[]{:S(2)}, u32[]{:S(2)}) %collective-permute-start.1) | collective-permute-done | bytes 24608 | tf_op jit(solution)/shard_map/ppermute | solution.py:18
  13.0 2.1 %collective-permute-start.2 = (bf16[192,128]{1,0:T(8,128)(2,1)S(1)}, bf16[192,128]{1,0:T(8,128)(2,1)S(1)}, u32[]{:S(2)}, u32[]{:S(2)}) collective-permute-start(bf16[192,128]{1,0:T(8,128)(2,1)S(1)} %maximum_select_fusion.2), channel_id=1, source_target_pairs={{0,4},{1,5},{2,6},{3,7},{4,0},{5,1},{6,2},{7,3},{8,12},{9,13},{10,... | collective-permute-start | bytes 147464 | tf_op jit(solution)/shard_map/ppermute | solution.py:18
  15.1 0.7 fusion.38.g_ref
  15.8 1.4 %collective-permute-done.2 = bf16[192,128]{1,0:T(8,128)(2,1)S(1)} collective-permute-done((bf16[192,128]{1,0:T(8,128)(2,1)S(1)}, bf16[192,128]{1,0:T(8,128)(2,1)S(1)}, u32[]{:S(2)}, u32[]{:S(2)}) %collective-permute-start.2) | collective-permute-done | bytes 49184 | tf_op jit(solution)/shard_map/ppermute | solution.py:18
  17.2 3.1 %collective-permute-start.3 = (bf16[384,128]{1,0:T(8,128)(2,1)S(1)}, bf16[384,128]{1,0:T(8,128)(2,1)S(1)}, u32[]{:S(2)}, u32[]{:S(2)}) collective-permute-start(bf16[384,128]{1,0:T(8,128)(2,1)S(1)} %maximum_select_fusion.1), channel_id=1, source_target_pairs={{0,8},{1,9},{2,10},{3,11},{4,12},{5,13},{6,14},{7,15},{8,0},{9,1},... | collective-permute-start | bytes 294920 | tf_op jit(solution)/shard_map/ppermute | solution.py:18
  20.3 0.6 fusion.39.limit_ref
  20.9 2.0 %collective-permute-done.3 = bf16[384,128]{1,0:T(8,128)(2,1)S(1)} collective-permute-done((bf16[384,128]{1,0:T(8,128)(2,1)S(1)}, bf16[384,128]{1,0:T(8,128)(2,1)S(1)}, u32[]{:S(2)}, u32[]{:S(2)}) %collective-permute-start.3) | collective-permute-done | bytes 98336 | tf_op jit(solution)/shard_map/ppermute | solution.py:18
  23.0 1.4 %fusion.30 = f32[768,3072]{1,0:T(8,128)S(1)} fusion(bf16[64,3072]{1,0:T(8,128)(2,1)S(1)} %copy-done.4, bf16[768,128]{1,0:T(8,128)(2,1)S(1)} %maximum_select_fusion, pred[]{:T(512)S(6)} %eq.27), kind=kOutput, calls=%fused_computation.50 | convolution fusion | flops 302039040 | bytes 10027009 | tf_op jit(solution)/shard_map/dot_general | solution.py:230
  24.4 1.5 %convert_reduce_fusion = (f32[768]{0:T(1024)S(1)}, bf16[768,3072]{1,0:T(8,128)(2,1)S(1)}) fusion(f32[768,3072]{1,0:T(8,128)S(1)} %fusion.30, bf16[64,3072]{1,0:T(8,128)(2,1)S(1)} %copy-done.5, bf16[768,128]{1,0:T(8,128)(2,1)S(1)} %maximum_select_fusion), kind=kOutput, calls=%fused_computation.3 | convolution fusion | flops 311426304 | bytes 14748672 | tf_op jit(solution)/shard_map/dot_general | solution.py:228
  25.9 1.4 %fusion.2 = f32[768]{0:T(1024)S(1)} fusion(bf16[768,3072]{1,0:T(8,128)(2,1)S(1)} %get-tuple-element.20, f32[768]{0:T(1024)S(1)} %broadcast_multiply_fusion), kind=kLoop, calls=%fused_computation.6 | loop fusion | flops 9436416 | bytes 4724736 | tf_op jit(solution)/shard_map/reduce_sum | solution.py:30
  27.3 4.8 %fusion.5.x_ref = bf16[768,3072]{1,0:T(8,128)(2,1)} fusion(bf16[768,3072]{1,0:T(8,128)(2,1)S(1)} %get-tuple-element.20, f32[3072]{0:T(1024)S(1)} %bitcast.47, f32[3072]{0:T(1024)S(1)} %bitcast.46, f32[768]{0:T(1024)S(1)} %add_rsqrt_fusion, f32[768]{0:T(1024)S(1)} %broadcast_multiply_fusion), kind=kLoop, calls=%fused_computation.9 | loop fusion | flops 14155776 | bytes 9467904 | tf_op jit(solution)/shard_map/convert_element_type | solution.py:32
  32.1 11.7 %shard_map.154.q_ref = bf16[768,1152]{1,0:T(8,128)(2,1)S(1)} custom-call(bf16[768,3072]{1,0:T(8,128)(2,1)} %fusion.5.x_ref, bf16[3072,1152]{1,0:T(8,128)(2,1)} %bitcast.51, f32[2,128]{1,0:T(2,128)S(1)} %fusion.38.g_ref), custom_call_target="tpu_custom_call" | custom-call | flops 5435817984 | bytes 13565952 | tf_op jit(solution)/shard_map/pallas_call | solution.py:74
  43.8 1.2 %copy-done.1 = bf16[768,1152]{1,0:T(8,128)(2,1)} copy-done((bf16[768,1152]{1,0:T(8,128)(2,1)}, bf16[768,1152]{1,0:T(8,128)(2,1)S(1)}, u32[]{:S(2)}) %copy-start.1) | copy-done | bytes 1769496
  45.1 1.6 %pad_maximum_fusion.m0_ref.m1_ref.m2_ref = bf16[1536,768]{1,0:T(8,128)(2,1)} fusion(bf16[768,768]{1,0:T(8,128)(2,1)S(1)} %bitcast.42, bf16[768,768]{1,0:T(8,128)(2,1)S(1)} %slice.94), kind=kLoop, calls=%fused_computation.20 | loop fusion | flops 4718592 | bytes 4718592 | tf_op jit(solution)/shard_map/concatenate | solution.py:256
  46.7 10.9 %shard_map.155 = bf16[768,384]{1,0:T(8,128)(2,1)} custom-call(s32[6,3]{1,0:T(8,128)} %bitcast_add_fusion.picked_ref, s32[6]{0:T(128)} %fusion.39.limit_ref, bf16[768,1152]{1,0:T(8,128)(2,1)} %copy-done.1, bf16[1536,768]{1,0:T(8,128)(2,1)} %pad_maximum_fusion.m0_ref.m1_ref.m2_ref, bf16[1536,768]{1,0:T(8,128)(2,1)} %pad_maximum_fusion.m0_ref.m1_ref.m2_ref, ...), custom_call_target="tpu_custom_call" | custom-call | flops 452984832 | bytes 4718592 | tf_op jit(solution)/shard_map/pallas_call | solution.py:133
  57.6 1.7 %gather_fusion.1 = bf16[16,48,384]{2,1,0:T(8,128)(2,1)S(1)} fusion(bf16[16,48,384]{2,1,0:T(8,128)(2,1)} %bitcast.41, s32[1024]{0:T(1024)S(1)} %pad_clamp_fusion), kind=kCustom, calls=%fused_computation.1 | custom fusion | bytes 1179712 | tf_op jit(solution)/shard_map/gather | solution.py:258
  59.4 2.8 %convolution_convert_fusion = bf16[768,3072]{1,0:T(8,128)(2,1)S(1)} fusion(bf16[768,384]{1,0:T(8,128)(2,1)S(1)} %bitcast.43, bf16[1,384,3072]{2,1,0:T(8,128)(2,1)S(1)} %copy-done), kind=kOutput, calls=%fused_computation.11 | convolution fusion | flops 1814298624 | bytes 7667712 | tf_op jit(solution)/shard_map/dot_general | solution.py:259
  62.2 0.2 slice.96
  62.5 4.5 %collective-permute-done.4 = bf16[384,3072]{1,0:T(8,128)(2,1)S(1)} collective-permute-done((bf16[384,3072]{1,0:T(8,128)(2,1)S(1)}, bf16[384,3072]{1,0:T(8,128)(2,1)S(1)}, u32[]{:S(2)}, u32[]{:S(2)}) %collective-permute-start.4) | collective-permute-done | bytes 2359328 | tf_op jit(solution)/shard_map/ppermute | solution.py:18
  67.0 1.0 fusion.43
  68.0 2.1 %collective-permute-start.5 = (bf16[96,3072]{1,0:T(8,128)(2,1)S(1)}, bf16[96,3072]{1,0:T(8,128)(2,1)S(1)}, u32[]{:S(2)}, u32[]{:S(2)}) collective-permute-start(bf16[96,3072]{1,0:T(8,128)(2,1)S(1)} %get-tuple-element.12), channel_id=1, source_target_pairs={{0,4},{1,5},{2,6},{3,7},{4,0},{5,1},{6,2},{7,3},{8,12},{9,13},{10,... | collective-permute-start | bytes 1769480 | tf_op jit(solution)/shard_map/ppermute | solution.py:18
  70.2 1.5 %collective-permute-start.7 = (bf16[96,3072]{1,0:T(8,128)(2,1)S(1)}, bf16[96,3072]{1,0:T(8,128)(2,1)S(1)}, u32[]{:S(2)}, u32[]{:S(2)}) collective-permute-start(bf16[96,3072]{1,0:T(8,128)(2,1)S(1)} %get-tuple-element.11), channel_id=1, source_target_pairs={{0,2},{1,3},{2,0},{3,1},{4,6},{5,7},{6,4},{7,5},{8,10},{9,11},{10,... | collective-permute-start | bytes 1769480 | tf_op jit(solution)/shard_map/ppermute | solution.py:18
  71.7 12.1 %collective-permute-done.5 = bf16[96,3072]{1,0:T(8,128)(2,1)S(1)} collective-permute-done((bf16[96,3072]{1,0:T(8,128)(2,1)S(1)}, bf16[96,3072]{1,0:T(8,128)(2,1)S(1)}, u32[]{:S(2)}, u32[]{:S(2)}) %collective-permute-start.5) | collective-permute-done | bytes 589856 | tf_op jit(solution)/shard_map/ppermute | solution.py:18
  83.8 1.5 %collective-permute-done.7 = bf16[96,3072]{1,0:T(8,128)(2,1)S(1)} collective-permute-done((bf16[96,3072]{1,0:T(8,128)(2,1)S(1)}, bf16[96,3072]{1,0:T(8,128)(2,1)S(1)}, u32[]{:S(2)}, u32[]{:S(2)}) %collective-permute-start.7) | collective-permute-done | bytes 589856 | tf_op jit(solution)/shard_map/ppermute | solution.py:18
  85.3 0.2 slice_add_fusion
  85.6 1.6 %collective-permute-start.6 = (bf16[48,3072]{1,0:T(8,128)(2,1)S(1)}, bf16[48,3072]{1,0:T(8,128)(2,1)S(1)}, u32[]{:S(2)}, u32[]{:S(2)}) collective-permute-start(bf16[48,3072]{1,0:T(8,128)(2,1)S(1)} %slice.128), channel_id=1, source_target_pairs={{0,2},{1,3},{2,0},{3,1},{4,6},{5,7},{6,4},{7,5},{8,10},{9,11},{10,... | collective-permute-start | bytes 884744 | tf_op jit(solution)/shard_map/ppermute | solution.py:18
  87.2 0.4 collective-permute-start.8
  87.6 5.9 %collective-permute-done.6 = bf16[48,3072]{1,0:T(8,128)(2,1)S(1)} collective-permute-done((bf16[48,3072]{1,0:T(8,128)(2,1)S(1)}, bf16[48,3072]{1,0:T(8,128)(2,1)S(1)}, u32[]{:S(2)}, u32[]{:S(2)}) %collective-permute-start.6) | collective-permute-done | bytes 294944 | tf_op jit(solution)/shard_map/ppermute | solution.py:18
  93.5 1.3 %collective-permute-done.8 = bf16[48,3072]{1,0:T(8,128)(2,1)S(1)} collective-permute-done((bf16[48,3072]{1,0:T(8,128)(2,1)S(1)}, bf16[48,3072]{1,0:T(8,128)(2,1)S(1)}, u32[]{:S(2)}, u32[]{:S(2)}) %collective-permute-start.8) | collective-permute-done | bytes 294944 | tf_op jit(solution)/shard_map/ppermute | solution.py:18
  94.9 0.8 select_convert_fusion
  95.7 3.4 %collective-permute-start.9 = (bf16[48,3072]{1,0:T(8,128)(2,1)}, bf16[48,3072]{1,0:T(8,128)(2,1)}, u32[]{:S(2)}, u32[]{:S(2)}) collective-permute-start(bf16[48,3072]{1,0:T(8,128)(2,1)} %select_convert_fusion), channel_id=1, source_target_pairs={{0,8},{1,9},{2,10},{3,11},{4,12},{5,13},{6,14},{7,15},{8,0},{9,1},... | collective-permute-start | bytes 884744 | tf_op jit(solution)/shard_map/ppermute | solution.py:18
  99.1 0.6 slice_add_fusion.4
  99.7 1.2 %fusion.35 = f32[48,3072]{1,0:T(8,128)S(1)} fusion(bf16[64,3072]{1,0:T(8,128)(2,1)} %param.21, bf16[768,128]{1,0:T(8,128)(2,1)} %copy-done.3, s32[]{:T(128)S(6)} %select_n.134), kind=kOutput, calls=%fused_computation.60 | convolution fusion | flops 18874368 | bytes 995332 | tf_op jit(solution)/shard_map/dot_general | solution.py:273
  101.0 9.8 %collective-permute-done.9 = bf16[48,3072]{1,0:T(8,128)(2,1)} collective-permute-done((bf16[48,3072]{1,0:T(8,128)(2,1)}, bf16[48,3072]{1,0:T(8,128)(2,1)}, u32[]{:S(2)}, u32[]{:S(2)}) %collective-permute-start.9) | collective-permute-done | bytes 294944 | tf_op jit(solution)/shard_map/ppermute | solution.py:18
  110.8 2.1 %convert_reduce_fusion.1 = (f32[48]{0:T(128)S(1)}, bf16[48,3072]{1,0:T(8,128)(2,1)S(1)}) fusion(f32[3072]{0:T(1024)} %bitcast.45, f32[48,3072]{1,0:T(8,128)S(1)} %fusion.35, bf16[64,3072]{1,0:T(8,128)(2,1)} %param.22, bf16[768,128]{1,0:T(8,128)(2,1)} %copy-done.3, s32[]{:T(128)S(6)} %select_n.134, s32[]{:T(128)S(6)} %add.186, f32[3072]{0:T(1024)} %bitcast.48, ...), kind=kOutput, calls=%fused_computation.25 | convolution fusion | flops 22413264 | bytes 3391689 | tf_op jit(solution)/shard_map/dot_general | solution.py:278
  112.8 0.3 fusion.15
  113.1 2.0 %fusion.24 = f32[48,64]{1,0:T(8,128)} fusion(bf16[3072,64]{0,1:T(8,128)(2,1)} %param.30, bf16[48,3072]{1,0:T(8,128)(2,1)S(1)} %get-tuple-element.22, f32[3072]{0:T(1024)} %bitcast.50, f32[3072]{0:T(1024)} %bitcast.49, f32[48]{0:T(128)S(1)} %add_rsqrt_fusion.1, f32[48]{0:T(128)S(1)} %broadcast_multiply_fusion.1), kind=kOutput, calls=%fused_computation.44 | convolution fusion | flops 19759104 | bytes 725376 | tf_op jit(solution)/shard_map/dot_general | solution.py:298
  (42 shorter events, 0.9 us)
Async XLA Ops:
  0.0 59.4 %copy-start = (bf16[1,384,3072]{2,1,0:T(8,128)(2,1)S(1)}, bf16[1,384,3072]{2,1,0:T(8,128)(2,1)}, u32[]{:S(2)}) copy-start(bf16[1,384,3072]{2,1,0:T(8,128)(2,1)} %param.26) | copy-start | bytes 7077892
  0.0 20.3 %copy-start.10 = (s32[2,6]{1,0:T(2,128)S(1)}, s32[2,6]{1,0:T(2,128)}, u32[]{:S(2)}) copy-start(s32[2,6]{1,0:T(2,128)} %param.20) | copy-start | bytes 148
  0.0 22.9 %copy-start.4 = (bf16[64,3072]{1,0:T(8,128)(2,1)S(1)}, bf16[64,3072]{1,0:T(8,128)(2,1)}, u32[]{:S(2)}) copy-start(bf16[64,3072]{1,0:T(8,128)(2,1)} %param.22) | copy-start | bytes 1179652
  1.0 6.7 %collective-permute-start = (bf16[48,128]{1,0:T(8,128)(2,1)S(1)}, bf16[48,128]{1,0:T(8,128)(2,1)S(1)}, u32[]{:S(2)}, u32[]{:S(2)}) collective-permute-start(bf16[48,128]{1,0:T(8,128)(2,1)S(1)} %pad_maximum_fusion.1), channel_id=1, source_target_pairs={{0,1},{1,0},{2,3},{3,2},{4,5},{5,4},{6,7},{7,6},{8,9},{9,8},{10,11... | collective-permute-start | bytes 36872 | tf_op jit(solution)/shard_map/ppermute | solution.py:18
  8.5 4.5 %collective-permute-start.1 = (bf16[96,128]{1,0:T(8,128)(2,1)S(1)}, bf16[96,128]{1,0:T(8,128)(2,1)S(1)}, u32[]{:S(2)}, u32[]{:S(2)}) collective-permute-start(bf16[96,128]{1,0:T(8,128)(2,1)S(1)} %maximum_select_fusion.3), channel_id=1, source_target_pairs={{0,2},{1,3},{2,0},{3,1},{4,6},{5,7},{6,4},{7,5},{8,10},{9,11},{10,... | collective-permute-start | bytes 73736 | tf_op jit(solution)/shard_map/ppermute | solution.py:18
  13.0 4.2 %collective-permute-start.2 = (bf16[192,128]{1,0:T(8,128)(2,1)S(1)}, bf16[192,128]{1,0:T(8,128)(2,1)S(1)}, u32[]{:S(2)}, u32[]{:S(2)}) collective-permute-start(bf16[192,128]{1,0:T(8,128)(2,1)S(1)} %maximum_select_fusion.2), channel_id=1, source_target_pairs={{0,4},{1,5},{2,6},{3,7},{4,0},{5,1},{6,2},{7,3},{8,12},{9,13},{10,... | collective-permute-start | bytes 147464 | tf_op jit(solution)/shard_map/ppermute | solution.py:18
  17.2 5.7 %collective-permute-start.3 = (bf16[384,128]{1,0:T(8,128)(2,1)S(1)}, bf16[384,128]{1,0:T(8,128)(2,1)S(1)}, u32[]{:S(2)}, u32[]{:S(2)}) collective-permute-start(bf16[384,128]{1,0:T(8,128)(2,1)S(1)} %maximum_select_fusion.1), channel_id=1, source_target_pairs={{0,8},{1,9},{2,10},{3,11},{4,12},{5,13},{6,14},{7,15},{8,0},{9,1},... | collective-permute-start | bytes 294920 | tf_op jit(solution)/shard_map/ppermute | solution.py:18
  23.0 1.5 %copy-start.3 = (bf16[768,128]{1,0:T(8,128)(2,1)}, bf16[768,128]{1,0:T(8,128)(2,1)S(1)}, u32[]{:S(2)}) copy-start(bf16[768,128]{1,0:T(8,128)(2,1)S(1)} %maximum_select_fusion) | copy-start | bytes 589828
  23.0 1.5 %copy-start.5 = (bf16[64,3072]{1,0:T(8,128)(2,1)S(1)}, bf16[64,3072]{1,0:T(8,128)(2,1)}, u32[]{:S(2)}) copy-start(bf16[64,3072]{1,0:T(8,128)(2,1)} %param.21) | copy-start | bytes 1179652
  32.1 13.0 %copy-start.8 = (bf16[1,768,768]{2,1,0:T(8,128)(2,1)S(1)}, bf16[1,768,768]{2,1,0:T(8,128)(2,1)}, u32[]{:S(2)}) copy-start(bf16[1,768,768]{2,1,0:T(8,128)(2,1)} %param.27) | copy-start | bytes 3538948
  43.8 1.2 %copy-start.1 = (bf16[768,1152]{1,0:T(8,128)(2,1)}, bf16[768,1152]{1,0:T(8,128)(2,1)S(1)}, u32[]{:S(2)}) copy-start(bf16[768,1152]{1,0:T(8,128)(2,1)S(1)} %shard_map.154.q_ref) | copy-start | bytes 5308420
  62.4 4.6 %collective-permute-start.4 = (bf16[384,3072]{1,0:T(8,128)(2,1)S(1)}, bf16[384,3072]{1,0:T(8,128)(2,1)S(1)}, u32[]{:S(2)}, u32[]{:S(2)}) collective-permute-start(bf16[384,3072]{1,0:T(8,128)(2,1)S(1)} %slice.96), channel_id=1, source_target_pairs={{0,1},{1,0},{2,3},{3,2},{4,5},{5,4},{6,7},{7,6},{8,9},{9,8},{10,11... | collective-permute-start | bytes 7077896 | tf_op jit(solution)/shard_map/ppermute | solution.py:18
  68.0 31.1 %copy-start.9 = (f32[2,3072]{1,0:T(2,128)S(1)}, f32[2,3072]{1,0:T(2,128)}, u32[]{:S(2)}) copy-start(f32[2,3072]{1,0:T(2,128)} %param.29) | copy-start | bytes 73732
  68.0 15.8 %collective-permute-start.5 = (bf16[96,3072]{1,0:T(8,128)(2,1)S(1)}, bf16[96,3072]{1,0:T(8,128)(2,1)S(1)}, u32[]{:S(2)}, u32[]{:S(2)}) collective-permute-start(bf16[96,3072]{1,0:T(8,128)(2,1)S(1)} %get-tuple-element.12), channel_id=1, source_target_pairs={{0,4},{1,5},{2,6},{3,7},{4,0},{5,1},{6,2},{7,3},{8,12},{9,13},{10,... | collective-permute-start | bytes 1769480 | tf_op jit(solution)/shard_map/ppermute | solution.py:18
  70.2 15.1 %collective-permute-start.7 = (bf16[96,3072]{1,0:T(8,128)(2,1)S(1)}, bf16[96,3072]{1,0:T(8,128)(2,1)S(1)}, u32[]{:S(2)}, u32[]{:S(2)}) collective-permute-start(bf16[96,3072]{1,0:T(8,128)(2,1)S(1)} %get-tuple-element.11), channel_id=1, source_target_pairs={{0,2},{1,3},{2,0},{3,1},{4,6},{5,7},{6,4},{7,5},{8,10},{9,11},{10,... | collective-permute-start | bytes 1769480 | tf_op jit(solution)/shard_map/ppermute | solution.py:18
  85.5 9.4 %copy-start.2 = (f32[96,3072]{1,0:T(8,128)}, f32[96,3072]{1,0:T(8,128)S(1)}, u32[]{:S(2)}) copy-start(f32[96,3072]{1,0:T(8,128)S(1)} %get-tuple-element.10) | copy-start | bytes 3538948
  85.6 8.0 %collective-permute-start.6 = (bf16[48,3072]{1,0:T(8,128)(2,1)S(1)}, bf16[48,3072]{1,0:T(8,128)(2,1)S(1)}, u32[]{:S(2)}, u32[]{:S(2)}) collective-permute-start(bf16[48,3072]{1,0:T(8,128)(2,1)S(1)} %slice.128), channel_id=1, source_target_pairs={{0,2},{1,3},{2,0},{3,1},{4,6},{5,7},{6,4},{7,5},{8,10},{9,11},{10,... | collective-permute-start | bytes 884744 | tf_op jit(solution)/shard_map/ppermute | solution.py:18
  87.2 7.7 %collective-permute-start.8 = (bf16[48,3072]{1,0:T(8,128)(2,1)S(1)}, bf16[48,3072]{1,0:T(8,128)(2,1)S(1)}, u32[]{:S(2)}, u32[]{:S(2)}) collective-permute-start(bf16[48,3072]{1,0:T(8,128)(2,1)S(1)} %slice.127), channel_id=1, source_target_pairs={{0,4},{1,5},{2,6},{3,7},{4,0},{5,1},{6,2},{7,3},{8,12},{9,13},{10,... | collective-permute-start | bytes 884744 | tf_op jit(solution)/shard_map/ppermute | solution.py:18
  93.5 2.2 %copy-start.6 = (bf16[48,3072]{1,0:T(8,128)(2,1)}, bf16[48,3072]{1,0:T(8,128)(2,1)S(1)}, u32[]{:S(2)}) copy-start(bf16[48,3072]{1,0:T(8,128)(2,1)S(1)} %collective-permute-done.6) | copy-start | bytes 884740
  94.9 4.2 %copy-start.7 = (bf16[48,3072]{1,0:T(8,128)(2,1)}, bf16[48,3072]{1,0:T(8,128)(2,1)S(1)}, u32[]{:S(2)}) copy-start(bf16[48,3072]{1,0:T(8,128)(2,1)S(1)} %collective-permute-done.8) | copy-start | bytes 884740
  95.7 15.0 %collective-permute-start.9 = (bf16[48,3072]{1,0:T(8,128)(2,1)}, bf16[48,3072]{1,0:T(8,128)(2,1)}, u32[]{:S(2)}, u32[]{:S(2)}) collective-permute-start(bf16[48,3072]{1,0:T(8,128)(2,1)} %select_convert_fusion), channel_id=1, source_target_pairs={{0,8},{1,9},{2,10},{3,11},{4,12},{5,13},{6,14},{7,15},{8,0},{9,1},... | collective-permute-start | bytes 884744 | tf_op jit(solution)/shard_map/ppermute | solution.py:18
